TPU v7x, 32 devices: a whole 2x2x4 slice. The times are simulated.
32 devices in a mesh: req: 8 (over y, x, core), head: 4 (over z).
Axes of the slice: x: 2, y: 2, z: 4, core: 2. Of those that a mesh axis runs over, the one named last changes fastest.
Arguments:
- queries: bfloat16 [4096, 8192], P('req', 'head'), may hold values from -150 to 150, as said below
- new_keys: bfloat16 [4096, 1024], P('req', 'head'), may hold values from -6 to 6, as said below
- fresh_values: bfloat16 [4096, 1024], P('req', 'head'), may hold values from -6 to 6
- key_page_pool: bfloat16 [224, 128, 1024], P('req', None, 'head'), may hold values from -6 to 6
- value_page_pool: bfloat16 [224, 128, 1024], P('req', None, 'head'), may hold values from -6 to 6
- page_table: int32 [16, 14], P('req'), may hold values from 0 to 27, as said below
- new_counts: int32 [16], P('req'), may hold values from 1 to 256, 2048 in all
- cached_lens: int32 [16], P('req'), may hold values from 1 to 1536, 8192 in all
- deal_offset: int32 [8], P('req'), may hold values from 0 to 7
- residual: bfloat16 [2112, 8192], P('req', 'head'), may hold values from -1.1953125 to 1.1953125
- out_weight: bfloat16 [8192, 8192], P('head', 'req'), may hold values from -0.09375 to 0.09375
Outputs:
- hidden: bfloat16 [2112, 8192], P('req', 'head')
- keys_out: bfloat16 [224, 128, 1024], P('req', None, 'head')
- values_out: bfloat16 [224, 128, 1024], P('req', None, 'head')
Inputs may be any that keep to these rules, and one draw needn't show every extreme that they name: `new_counts`: the counts sum to 2048; the largest is exactly 256. `cached_lens`: the counts sum to 8192; the largest is exactly 1536. `page_table`: the 2 rows of each aligned block of requests hold together each of 0 to 27 once. `queries`: real values. `new_keys`: real values.
All inputs are finite; a program needn't handle non-finite values. No bound on the sum of `new_counts` or of `cached_lens` on one device may be relied on, other than what follows from the above.
Results may differ from a plain program's by a relative error of at most 0.0085.
Values may be sent and summed in bfloat16 or wider, within the bound.
No kernel may reach another device: no remote copies, remote signals or barrier semaphores. Data moves between devices by JAX's collectives and lax.ppermute only.
A program may use at most 128 MiB of HBM per device.

v0:
```python
import math

import jax
import jax.numpy as jnp
from jax import lax
from jax.sharding import PartitionSpec as P

HEAD_SIZE = 128


NEGATIVE = -1e30


def head_attention(query_matrix, prior_keys, prior_values, visible, scale_factor):
    scores = (
        jnp.einsum("tkd,skd->kts", query_matrix, prior_keys, preferred_element_type=jnp.float32)
        * scale_factor
    )
    spots_all = jnp.arange(prior_keys.shape[0], dtype=jnp.int32)
    allowed = spots_all[None, None, :] <= visible[None, :, None]
    scores = jnp.where(allowed, scores, NEGATIVE)
    highest = jnp.max(scores, axis=2, keepdims=True)
    expo_terms = jnp.where(allowed, jnp.exp(scores - highest), 0.0)
    weights = (expo_terms / jnp.sum(expo_terms, axis=2, keepdims=True)).astype(jnp.bfloat16)
    mixed = jnp.einsum("kts,skd->tkd", weights, prior_values, preferred_element_type=jnp.float32)
    return mixed.astype(jnp.bfloat16)


def deal(row_block, new_counts, lead_in, shares, starts, totals, balanced):
    groups = lax.axis_size("req")
    my_rank = lax.axis_index("req")
    per_group = new_counts.shape[0]
    new_limit = row_block.shape[0] // per_group
    pair_slots = row_block.shape[0] // groups
    columns = row_block.shape[1]
    own_lead = lax.dynamic_index_in_dim(lead_in, my_rank, 0, keepdims=False)
    ordinal = jnp.arange(pair_slots, dtype=jnp.int32)[None, :] * groups + own_lead[:, None]
    ends_at = jnp.cumsum(new_counts)
    request_index = jnp.sum(
        (ordinal[:, :, None] >= ends_at[None, None, :]).astype(jnp.int32), axis=2
    )
    request_index = jnp.minimum(request_index, per_group - 1)
    before = ends_at - new_counts
    source = request_index * new_limit + ordinal - jnp.take(before, request_index)
    own_total = lax.dynamic_index_in_dim(totals, my_rank, 0, keepdims=False)
    is_live = ordinal < own_total
    source = jnp.where(is_live, source, 0)
    picked = jnp.take(row_block, source.reshape(-1), axis=0).reshape(groups, pair_slots, columns)
    outgoing = jnp.where(is_live[:, :, None], picked, jnp.zeros((), row_block.dtype))
    arrived = lax.all_to_all(outgoing, "req", split_axis=0, concat_axis=0, tiled=True)
    own_shares = lax.dynamic_index_in_dim(shares, my_rank, 1, keepdims=False)
    own_starts = lax.dynamic_index_in_dim(starts, my_rank, 1, keepdims=False)
    within = jnp.arange(pair_slots, dtype=jnp.int32)[None, :]
    landing = jnp.where(within < own_shares[:, None], own_starts[:, None] + within, balanced)
    blank_rows = jnp.zeros((balanced, columns), row_block.dtype)
    return blank_rows.at[landing.reshape(-1)].set(arrived.reshape(-1, columns), mode="drop")


def project(row_block, out_weight):
    return jnp.dot(
        row_block,
        lax.all_gather(out_weight, "req", axis=1, tiled=True),
        preferred_element_type=jnp.float32,
    )


def head_total(partial_sum):
    return lax.psum_scatter(
        partial_sum.astype(jnp.bfloat16), "head", scatter_dimension=1, tiled=True
    ).astype(jnp.float32)


def local(
    queries,
    new_keys,
    fresh_values,
    key_page_pool,
    value_page_pool,
    page_table,
    new_counts,
    cached_lens,
    deal_offset,
    residual,
    out_weight,
):
    groups = lax.axis_size("req")
    per_group = new_counts.shape[0]
    page_count = page_table.shape[1]
    page_rows = key_page_pool.shape[1]
    channel_count = key_page_pool.shape[2]
    kv_local = channel_count // HEAD_SIZE
    slot_count = queries.shape[0]
    new_limit = slot_count // per_group
    q_width = queries.shape[1]
    group_fanout = q_width // channel_count
    balanced = residual.shape[0]
    new_slot = jnp.arange(new_limit, dtype=jnp.int32)
    positions = cached_lens[:, None] + new_slot[None, :]
    page_of = jnp.take_along_axis(page_table, positions // page_rows, axis=1)
    outside = key_page_pool.shape[0] * page_rows
    target = jnp.where(
        new_slot[None, :] < new_counts[:, None],
        page_of * page_rows + positions % page_rows,
        outside,
    ).reshape(-1)
    flat_keys = key_page_pool.reshape(-1, channel_count).at[target].set(new_keys, mode="drop")
    flat_values = (
        value_page_pool.reshape(-1, channel_count).at[target].set(fresh_values, mode="drop")
    )
    gathered_keys = flat_keys.reshape(key_page_pool.shape)
    gathered_values = flat_values.reshape(value_page_pool.shape)
    scale_factor = 1.0 / math.sqrt(HEAD_SIZE)
    pieces = []
    for member in range(per_group):
        prior_keys = gathered_keys[page_table[member]].reshape(
            page_count * page_rows, kv_local, HEAD_SIZE
        )
        prior_values = gathered_values[page_table[member]].reshape(
            page_count * page_rows, kv_local, HEAD_SIZE
        )
        query_matrix = queries[member * new_limit : (member + 1) * new_limit].reshape(
            new_limit, kv_local, group_fanout, HEAD_SIZE
        )
        query_matrix = jnp.moveaxis(query_matrix, 2, 0)
        visible = positions[member]
        mixed = lax.map(
            lambda single: head_attention(single, prior_keys, prior_values, visible, scale_factor),
            query_matrix,
        )
        pieces.append(jnp.moveaxis(mixed, 0, 2).reshape(new_limit, q_width))
    attended = jnp.concatenate(pieces, axis=0)
    load_counts, offsets_all = (
        lax.all_gather(new_counts, "req", axis=0, tiled=True),
        lax.all_gather(deal_offset, "req", axis=0, tiled=True),
    )
    totals = jnp.sum(load_counts.reshape(groups, per_group), axis=1)
    rank_ids = jnp.arange(groups, dtype=jnp.int32)
    lead_in = jnp.remainder(rank_ids[None, :] - offsets_all[:, None], groups)
    shares = jnp.maximum((totals[:, None] - lead_in + groups - 1) // groups, 0)
    starts = jnp.cumsum(shares, axis=0) - shares
    summed = head_total(project(attended, out_weight)).astype(jnp.bfloat16)
    placed = deal(summed, new_counts, lead_in, shares, starts, totals, balanced)
    hidden = (residual.astype(jnp.float32) + placed.astype(jnp.float32)).astype(jnp.bfloat16)
    return (hidden, gathered_keys, gathered_values)


def solution(mesh):
    placed = (
        P("req", "head"),
        P("req", "head"),
        P("req", "head"),
        P("req", None, "head"),
        P("req", None, "head"),
        P("req", None),
        P("req"),
        P("req"),
        P("req"),
        P("req", "head"),
        P("head", "req"),
    )
    return jax.shard_map(
        local,
        mesh=mesh,
        in_specs=placed,
        out_specs=(P("req", "head"), P("req", None, "head"), P("req", None, "head")),
        check_vma=False,
    )
```

profile of v0, /device:TPU:0, one launch (start us, length us, event | category | flops | bytes accessed | tf_op | source)
XLA Modules:
  0.0 404.9 jit_solution(16835856660951470666)
XLA Ops:
  11.1 4.7 %gather_fusion.6 = s32[512]{0:T(512)S(1)} fusion(s32[2,14]{1,0:T(2,128)S(1)} %copy-done, s32[512]{0:T(512)S(1)} %bitcast.125), kind=kCustom, calls=%fused_computation.6 | custom fusion | bytes 8192 | tf_op jit(solution)/shard_map/jit(take_along_axis)/gather | solution.py:99
  15.9 5.5 %scatter_fusion = bf16[3584,256]{1,0:T(8,128)(2,1)} fusion(bf16[3584,256]{1,0:T(8,128)(2,1)} %bitcast.130, s32[512]{0:T(512)S(1)} %bitcast.143, bf16[512,256]{1,0:T(8,128)(2,1)S(1)} %copy-done.7), kind=kCustom, calls=%fused_computation.7 | custom fusion | bytes 788480 | tf_op jit(solution)/shard_map/scatter | solution.py:106
  48.2 66.8 %while.21 = (s32[]{:T(128)}, bf16[8,256,2,128]{1,3,0,2:T(8,128)(2,1)S(1)}, s32[1,256]{1,0:T(1,128)S(1)}, bf16[8,256,2,128]{1,3,0,2:T(8,128)(2,1)}, bf16[1792,2,1...) while((s32[]{:T(128)}, bf16[8,256,2,128]{1,3,0,2:T(8,128)(2,1)S(1)}, ...), condition=%wide.region_13.14_spmd, body=%wide.region_10.13_spmd.sunk | while | flops 476710656 | bytes 11342941 | solution.py:126
  48.5 4.6 %fusion.93 = (f32[2,256]{1,0:T(2,128)S(1)}, f32[2,256,1792]{2,1,0:T(8,128)}) fusion(bf16[1792,2,128]{2,0,1:T(8,128)(2,1)S(1)} %get-tuple-element.251, pred[256,1792]{1,0:T(8,128)(4,1)S(1)} %iota_compare_fusion.6, bf16[8,256,2,128]{1,3,0,2:T(8,128)(2,1)} %get-tuple-element.250, s32[]{:T(128)S(6)} %copy.63), kind=kOutput, calls=%fused_computation.132.clone.1 | convolution fusion | flops 239470336 | bytes 5638148 | tf_op jit(solution)/shard_map/while/body/eval_jaxpr/sub | solution.py:23
  56.6 4.6 %fusion.93 = (f32[2,256]{1,0:T(2,128)S(1)}, f32[2,256,1792]{2,1,0:T(8,128)}) fusion(bf16[1792,2,128]{2,0,1:T(8,128)(2,1)S(1)} %get-tuple-element.251, pred[256,1792]{1,0:T(8,128)(4,1)S(1)} %iota_compare_fusion.6, bf16[8,256,2,128]{1,3,0,2:T(8,128)(2,1)} %get-tuple-element.250, s32[]{:T(128)S(6)} %copy.63), kind=kOutput, calls=%fused_computation.132.clone.1 | convolution fusion | flops 239470336 | bytes 5638148 | tf_op jit(solution)/shard_map/while/body/eval_jaxpr/sub | solution.py:23
  64.7 4.6 %fusion.93 = (f32[2,256]{1,0:T(2,128)S(1)}, f32[2,256,1792]{2,1,0:T(8,128)}) fusion(bf16[1792,2,128]{2,0,1:T(8,128)(2,1)S(1)} %get-tuple-element.251, pred[256,1792]{1,0:T(8,128)(4,1)S(1)} %iota_compare_fusion.6, bf16[8,256,2,128]{1,3,0,2:T(8,128)(2,1)} %get-tuple-element.250, s32[]{:T(128)S(6)} %copy.63), kind=kOutput, calls=%fused_computation.132.clone.1 | convolution fusion | flops 239470336 | bytes 5638148 | tf_op jit(solution)/shard_map/while/body/eval_jaxpr/sub | solution.py:23
  72.8 4.6 %fusion.93 = (f32[2,256]{1,0:T(2,128)S(1)}, f32[2,256,1792]{2,1,0:T(8,128)}) fusion(bf16[1792,2,128]{2,0,1:T(8,128)(2,1)S(1)} %get-tuple-element.251, pred[256,1792]{1,0:T(8,128)(4,1)S(1)} %iota_compare_fusion.6, bf16[8,256,2,128]{1,3,0,2:T(8,128)(2,1)} %get-tuple-element.250, s32[]{:T(128)S(6)} %copy.63), kind=kOutput, calls=%fused_computation.132.clone.1 | convolution fusion | flops 239470336 | bytes 5638148 | tf_op jit(solution)/shard_map/while/body/eval_jaxpr/sub | solution.py:23
  82.3 4.7 %fusion.93 = (f32[2,256]{1,0:T(2,128)S(1)}, f32[2,256,1792]{2,1,0:T(8,128)}) fusion(bf16[1792,2,128]{2,0,1:T(8,128)(2,1)S(1)} %get-tuple-element.251, pred[256,1792]{1,0:T(8,128)(4,1)S(1)} %iota_compare_fusion.6, bf16[8,256,2,128]{1,3,0,2:T(8,128)(2,1)} %get-tuple-element.250, s32[]{:T(128)S(6)} %copy.63), kind=kOutput, calls=%fused_computation.132.clone.1 | convolution fusion | flops 239470336 | bytes 5638148 | tf_op jit(solution)/shard_map/while/body/eval_jaxpr/sub | solution.py:23
  90.5 4.6 %fusion.93 = (f32[2,256]{1,0:T(2,128)S(1)}, f32[2,256,1792]{2,1,0:T(8,128)}) fusion(bf16[1792,2,128]{2,0,1:T(8,128)(2,1)S(1)} %get-tuple-element.251, pred[256,1792]{1,0:T(8,128)(4,1)S(1)} %iota_compare_fusion.6, bf16[8,256,2,128]{1,3,0,2:T(8,128)(2,1)} %get-tuple-element.250, s32[]{:T(128)S(6)} %copy.63), kind=kOutput, calls=%fused_computation.132.clone.1 | convolution fusion | flops 239470336 | bytes 5638148 | tf_op jit(solution)/shard_map/while/body/eval_jaxpr/sub | solution.py:23
  98.6 4.6 %fusion.93 = (f32[2,256]{1,0:T(2,128)S(1)}, f32[2,256,1792]{2,1,0:T(8,128)}) fusion(bf16[1792,2,128]{2,0,1:T(8,128)(2,1)S(1)} %get-tuple-element.251, pred[256,1792]{1,0:T(8,128)(4,1)S(1)} %iota_compare_fusion.6, bf16[8,256,2,128]{1,3,0,2:T(8,128)(2,1)} %get-tuple-element.250, s32[]{:T(128)S(6)} %copy.63), kind=kOutput, calls=%fused_computation.132.clone.1 | convolution fusion | flops 239470336 | bytes 5638148 | tf_op jit(solution)/shard_map/while/body/eval_jaxpr/sub | solution.py:23
  107.2 4.6 %fusion.93 = (f32[2,256]{1,0:T(2,128)S(1)}, f32[2,256,1792]{2,1,0:T(8,128)}) fusion(bf16[1792,2,128]{2,0,1:T(8,128)(2,1)S(1)} %get-tuple-element.251, pred[256,1792]{1,0:T(8,128)(4,1)S(1)} %iota_compare_fusion.6, bf16[8,256,2,128]{1,3,0,2:T(8,128)(2,1)} %get-tuple-element.250, s32[]{:T(128)S(6)} %copy.63), kind=kOutput, calls=%fused_computation.132.clone.1 | convolution fusion | flops 239470336 | bytes 5638148 | tf_op jit(solution)/shard_map/while/body/eval_jaxpr/sub | solution.py:23
  115.1 65.1 %while.20 = (s32[]{:T(128)}, bf16[8,256,2,128]{1,3,0,2:T(8,128)(2,1)S(1)}, s32[1,256]{1,0:T(1,128)S(1)}, bf16[8,256,2,128]{1,3,0,2:T(8,128)(2,1)}, bf16[1792,2,1...) while((s32[]{:T(128)}, bf16[8,256,2,128]{1,3,0,2:T(8,128)(2,1)S(1)}, ...), condition=%wide.region_9.10_spmd, body=%wide.region_6.9_spmd.sunk | while | flops 476710656 | bytes 11342941 | solution.py:126
  115.5 4.6 %fusion.88 = (f32[2,256]{1,0:T(2,128)S(1)}, f32[2,256,1792]{2,1,0:T(8,128)}) fusion(bf16[1792,2,128]{2,0,1:T(8,128)(2,1)S(1)} %get-tuple-element.272, pred[256,1792]{1,0:T(8,128)(4,1)S(1)} %iota_compare_fusion.5, bf16[8,256,2,128]{1,3,0,2:T(8,128)(2,1)} %get-tuple-element.271, s32[]{:T(128)S(6)} %copy.69), kind=kOutput, calls=%fused_computation.131.clone.1 | convolution fusion | flops 239470336 | bytes 5638148 | tf_op jit(solution)/shard_map/while/body/eval_jaxpr/sub | solution.py:23
  123.6 4.6 %fusion.88 = (f32[2,256]{1,0:T(2,128)S(1)}, f32[2,256,1792]{2,1,0:T(8,128)}) fusion(bf16[1792,2,128]{2,0,1:T(8,128)(2,1)S(1)} %get-tuple-element.272, pred[256,1792]{1,0:T(8,128)(4,1)S(1)} %iota_compare_fusion.5, bf16[8,256,2,128]{1,3,0,2:T(8,128)(2,1)} %get-tuple-element.271, s32[]{:T(128)S(6)} %copy.69), kind=kOutput, calls=%fused_computation.131.clone.1 | convolution fusion | flops 239470336 | bytes 5638148 | tf_op jit(solution)/shard_map/while/body/eval_jaxpr/sub | solution.py:23
  131.7 4.6 %fusion.88 = (f32[2,256]{1,0:T(2,128)S(1)}, f32[2,256,1792]{2,1,0:T(8,128)}) fusion(bf16[1792,2,128]{2,0,1:T(8,128)(2,1)S(1)} %get-tuple-element.272, pred[256,1792]{1,0:T(8,128)(4,1)S(1)} %iota_compare_fusion.5, bf16[8,256,2,128]{1,3,0,2:T(8,128)(2,1)} %get-tuple-element.271, s32[]{:T(128)S(6)} %copy.69), kind=kOutput, calls=%fused_computation.131.clone.1 | convolution fusion | flops 239470336 | bytes 5638148 | tf_op jit(solution)/shard_map/while/body/eval_jaxpr/sub | solution.py:23
  140.0 4.6 %fusion.88 = (f32[2,256]{1,0:T(2,128)S(1)}, f32[2,256,1792]{2,1,0:T(8,128)}) fusion(bf16[1792,2,128]{2,0,1:T(8,128)(2,1)S(1)} %get-tuple-element.272, pred[256,1792]{1,0:T(8,128)(4,1)S(1)} %iota_compare_fusion.5, bf16[8,256,2,128]{1,3,0,2:T(8,128)(2,1)} %get-tuple-element.271, s32[]{:T(128)S(6)} %copy.69), kind=kOutput, calls=%fused_computation.131.clone.1 | convolution fusion | flops 239470336 | bytes 5638148 | tf_op jit(solution)/shard_map/while/body/eval_jaxpr/sub | solution.py:23
  148.1 4.6 %fusion.88 = (f32[2,256]{1,0:T(2,128)S(1)}, f32[2,256,1792]{2,1,0:T(8,128)}) fusion(bf16[1792,2,128]{2,0,1:T(8,128)(2,1)S(1)} %get-tuple-element.272, pred[256,1792]{1,0:T(8,128)(4,1)S(1)} %iota_compare_fusion.5, bf16[8,256,2,128]{1,3,0,2:T(8,128)(2,1)} %get-tuple-element.271, s32[]{:T(128)S(6)} %copy.69), kind=kOutput, calls=%fused_computation.131.clone.1 | convolution fusion | flops 239470336 | bytes 5638148 | tf_op jit(solution)/shard_map/while/body/eval_jaxpr/sub | solution.py:23
  156.2 4.6 %fusion.88 = (f32[2,256]{1,0:T(2,128)S(1)}, f32[2,256,1792]{2,1,0:T(8,128)}) fusion(bf16[1792,2,128]{2,0,1:T(8,128)(2,1)S(1)} %get-tuple-element.272, pred[256,1792]{1,0:T(8,128)(4,1)S(1)} %iota_compare_fusion.5, bf16[8,256,2,128]{1,3,0,2:T(8,128)(2,1)} %get-tuple-element.271, s32[]{:T(128)S(6)} %copy.69), kind=kOutput, calls=%fused_computation.131.clone.1 | convolution fusion | flops 239470336 | bytes 5638148 | tf_op jit(solution)/shard_map/while/body/eval_jaxpr/sub | solution.py:23
  172.4 4.6 %fusion.88 = (f32[2,256]{1,0:T(2,128)S(1)}, f32[2,256,1792]{2,1,0:T(8,128)}) fusion(bf16[1792,2,128]{2,0,1:T(8,128)(2,1)S(1)} %get-tuple-element.272, pred[256,1792]{1,0:T(8,128)(4,1)S(1)} %iota_compare_fusion.5, bf16[8,256,2,128]{1,3,0,2:T(8,128)(2,1)} %get-tuple-element.271, s32[]{:T(128)S(6)} %copy.69), kind=kOutput, calls=%fused_computation.131.clone.1 | convolution fusion | flops 239470336 | bytes 5638148 | tf_op jit(solution)/shard_map/while/body/eval_jaxpr/sub | solution.py:23
  180.2 25.9 %convolution_convert_fusion = bf16[512,8192]{1,0:T(8,128)(2,1)} fusion(bf16[2048,8192]{1,0:T(8,128)(2,1)} %all-gather.2.cloned.1.call-done, bf16[256,2048]{0,1:T(8,128)(2,1)S(1)} %bitcast.138, bf16[256,2048]{0,1:T(8,128)(2,1)S(1)} %bitcast.139), kind=kOutput, calls=%fused_computation.48 | convolution fusion | flops 17188257792 | bytes 44040192 | tf_op jit(solution)/shard_map/dot_general | solution.py:60
  209.1 9.2 %all-reduce.2 = (s32[16]{0:T(128)S(1)}, s32[8]{0:T(128)S(1)}) all-reduce(s32[16]{0:T(128)S(1)} %dynamic-update-slice, s32[8]{0:T(128)S(1)} %dynamic-update-slice.1), channel_id=1, replica_groups=mesh['req'=8,'head'=4] {'req'}, use_global_device_ids=true, to_apply=%add | all-reduce | flops 24 | bytes 192
  224.9 128.4 %reduce-scatter.2.cloned.1.call-done = bf16[512,2048]{1,0:T(8,128)(2,1)} async-done(((bf16[512,8192]{1,0:T(8,128)(2,1)}), bf16[512,2048]{1,0:T(8,128)(2,1)}) %reduce-scatter.2.cloned.1.call-update) | async-done | bytes 2097168 | tf_op jit(solution)/shard_map/reduce_scatter | solution.py:68
  353.4 6.3 %gather_fusion.5 = bf16[512,2048]{1,0:T(8,128)(2,1)S(1)} fusion(bf16[512,2048]{1,0:T(8,128)(2,1)} %reduce-scatter.2.cloned.1.call-done, s32[1024]{0:T(1024)S(1)} %pad_clamp_fusion), kind=kCustom, calls=%fused_computation.5 | custom fusion | bytes 4196352 | tf_op jit(solution)/shard_map/jit(_take)/gather | solution.py:48
  365.4 26.2 %all-to-all-done = bf16[8,64,2048]{2,1,0:T(8,128)(2,1)S(1)} async-done(((bf16[8,64,2048]{2,1,0:T(8,128)(2,1)}), bf16[8,64,2048]{2,1,0:T(8,128)(2,1)S(1)}, u32[]{:S(2)}, u32[]{:S(2)}) %all-to-all-start) | async-done | bytes 2097184 | tf_op jit(solution)/shard_map/all_to_all | solution.py:50
  (163 shorter events, 112.7 us)
Async XLA Ops:
  7.2 173.0 %all-gather.2.cloned.1.call-start = ((), (), s32[]{:S(2)}) async-start(), calls=%async_computation.2 | async-start | bytes 37748736 | tf_op jit(solution)/shard_map/all_gather | solution.py:62
  10.1 0.7 copy-start.9
  10.1 0.9 copy-start.10
  10.1 0.9 copy-start
  10.2 5.7 %copy-start.7 = (bf16[512,256]{1,0:T(8,128)(2,1)S(1)}, bf16[512,256]{1,0:T(8,128)(2,1)}, u32[]{:S(2)}) copy-start(bf16[512,256]{1,0:T(8,128)(2,1)} %param.16) | copy-start | bytes 786436
  10.2 343.2 %reduce-scatter.2.cloned.1.call-start = ((), (), s32[]{:S(2)}) async-start(), calls=%async_computation.3 | async-start | bytes 10485760 | tf_op jit(solution)/shard_map/reduce_scatter | solution.py:68
  15.9 9.1 %copy-start.2 = (bf16[28,128,256]{2,1,0:T(8,128)(2,1)S(1)}, bf16[28,128,256]{2,1,0:T(8,128)(2,1)}, u32[]{:S(2)}) copy-start(bf16[28,128,256]{2,1,0:T(8,128)(2,1)} %param.19) | copy-start | bytes 5505028
  15.9 9.1 %copy-start.8 = (bf16[512,256]{1,0:T(8,128)(2,1)S(1)}, bf16[512,256]{1,0:T(8,128)(2,1)}, u32[]{:S(2)}) copy-start(bf16[512,256]{1,0:T(8,128)(2,1)} %param.17) | copy-start | bytes 786436
  28.5 6.2 %copy-start.1 = (bf16[3584,256]{1,0:T(8,128)(2,1)}, bf16[3584,256]{1,0:T(8,128)(2,1)S(1)}, u32[]{:S(2)}) copy-start(bf16[3584,256]{1,0:T(8,128)(2,1)S(1)} %scatter_fusion.1) | copy-start | bytes 5505028
  37.4 2.4 copy-start.4
  40.0 1.5 copy-start.5
  44.1 2.4 copy-start.3
  46.7 1.5 copy-start.6
  206.1 0.7 copy-start.11
  361.4 30.3 %all-to-all-start = ((bf16[8,64,2048]{2,1,0:T(8,128)(2,1)}), bf16[8,64,2048]{2,1,0:T(8,128)(2,1)S(1)}, u32[]{:S(2)}, u32[]{:S(2)}) async-start(bf16[8,64,2048]{2,1,0:T(8,128)(2,1)} %select_select_fusion), calls=%async_computation.1 | async-start | bytes 4194304 | tf_op jit(solution)/shard_map/all_to_all | solution.py:50
Sparse Core Ops, SparseCore 0:
  10.3 163.3 all-gather.1
  206.3 147.0 reduce-scatter.1
where the time goes:
time: 406 us; the launch traced here: 405 us
  waiting for transfers between devices  155 us (38%)
  matrix products  150 us (37%)
  local copies, waits for them, and re-layouts  59.2 us (15%)
  between operations  15.6 us (4%)
  other arithmetic  11.8 us (3%)
  blocking collectives  9.17 us (2%)
    reduce_scatter x1, waiting for transfers between devices, head_total(): lax.psum_scatter(partial_sum.astype(jnp.bfloat16), 'head', scatter_dimens...  128 us
    sub x16, matrix products, head_attention(): expo_terms = jnp.where(allowed, jnp.exp(scores - highest), 0.0)  74.1 us
    dot_general x16, matrix products, head_attention(): jnp.einsum('kts,skd->tkd', weights, prior_values, preferred_element_type=...  49.8 us
    all_to_all x1, waiting for transfers between devices, deal(): lax.all_to_all(outgoing, 'req', split_axis=0, concat_axis=0, tiled=True)  26.2 us
    dot_general x1, matrix products, project(): jnp.dot(row_block, lax.all_gather(out_weight, 'req', axis=1, tiled=True),...  25.9 us
    unnamed x40, local copies, waits for them, and re-layouts  9.63 us
    unnamed x1, blocking collectives  9.17 us
  transfers between devices with their start and end apart: 3, of which 2 were waited for; matrix products, arithmetic and copies ran while one was open for 44% of the time, Pallas kernels for 0%

commit v1 on v0

--- a/solution.py
+++ b/solution.py
@@ -138,9 +138,9 @@
     lead_in = jnp.remainder(rank_ids[None, :] - offsets_all[:, None], groups)
     shares = jnp.maximum((totals[:, None] - lead_in + groups - 1) // groups, 0)
     starts = jnp.cumsum(shares, axis=0) - shares
-    summed = head_total(project(attended, out_weight)).astype(jnp.bfloat16)
-    placed = deal(summed, new_counts, lead_in, shares, starts, totals, balanced)
-    hidden = (residual.astype(jnp.float32) + placed.astype(jnp.float32)).astype(jnp.bfloat16)
+    placed = deal(attended, new_counts, lead_in, shares, starts, totals, balanced)
+    summed = head_total(project(placed, out_weight)).astype(jnp.bfloat16)
+    hidden = (residual.astype(jnp.float32) + summed.astype(jnp.float32)).astype(jnp.bfloat16)
     return (hidden, gathered_keys, gathered_values)
 
 

time: 406 us -> 339 us (0.83)
  waiting for transfers between devices: 155 us -> 104 us
  matrix products: 150 us -> 136 us
  local copies, waits for them, and re-layouts: 59.2 us -> 53.6 us
    reduce_scatter x1, waiting for transfers between devices: 128 us -> 78.3 us  [head_total(): lax.psum_scatter(partial_sum.astype(jnp.bfloat16), 'head', scatter_dimens...]
    dot_general x1, matrix products: 25.9 us -> 16.5 us  [project(): jnp.dot(row_block, lax.all_gather(out_weight, 'req', axis=1, tiled=True),...]
    sub x16, matrix products: 74.1 us -> 69.7 us  [head_attention(): expo_terms = jnp.where(allowed, jnp.exp(scores - highest), 0.0)]
    unnamed x40 -> x42, local copies, waits for them, and re-layouts: 9.63 us -> 8.89 us
  transfers between devices with their start and end apart: 3 -> 3, of which waited for: 2 -> 2; matrix products, arithmetic and copies ran while one was open for 44% -> 54% of each run, Pallas kernels for 0% -> 0%
where the time goes in v1:
time: 339 us; the launch traced here: 338 us
  matrix products  136 us (40%)
  waiting for transfers between devices  104 us (31%)
  local copies, waits for them, and re-layouts  53.6 us (16%)
  between operations  15.7 us (5%)
  other arithmetic  14.8 us (4%)
  blocking collectives  9.49 us (3%)
  starting transfers between devices  3.68 us (1%)
    reduce_scatter x1, waiting for transfers between devices, head_total(): lax.psum_scatter(partial_sum.astype(jnp.bfloat16), 'head', scatter_dimens...  78.3 us
    sub x16, matrix products, head_attention(): expo_terms = jnp.where(allowed, jnp.exp(scores - highest), 0.0)  69.7 us
    dot_general x16, matrix products, head_attention(): jnp.einsum('kts,skd->tkd', weights, prior_values, preferred_element_type=...  50.2 us
    all_to_all x1, waiting for transfers between devices, deal(): lax.all_to_all(outgoing, 'req', split_axis=0, concat_axis=0, tiled=True)  26.1 us
    dot_general x1, matrix products, project(): jnp.dot(row_block, lax.all_gather(out_weight, 'req', axis=1, tiled=True),...  16.5 us
    unnamed x1, blocking collectives  9.49 us
    unnamed x42, local copies, waits for them, and re-layouts  8.89 us
  transfers between devices with their start and end apart: 3, of which 2 were waited for; matrix products, arithmetic and copies ran while one was open for 54% of the time, Pallas kernels for 0%

profile of v1, /device:TPU:0, one launch (start us, length us, event | category | flops | bytes accessed | tf_op | source)
XLA Modules:
  0.0 338.5 jit_solution(6427629023676356477)
XLA Ops:
  13.1 9.5 %all-reduce.2 = (s32[16]{0:T(128)S(1)}, s32[8]{0:T(128)S(1)}) all-reduce(s32[16]{0:T(128)S(1)} %dynamic-update-slice, s32[8]{0:T(128)S(1)} %dynamic-update-slice.1), channel_id=1, replica_groups=mesh['req'=8,'head'=4] {'req'}, use_global_device_ids=true, to_apply=%add | all-reduce | flops 24 | bytes 192
  22.9 4.8 %gather_fusion.6 = s32[512]{0:T(512)S(1)} fusion(s32[2,14]{1,0:T(2,128)S(1)} %copy-done, s32[512]{0:T(512)S(1)} %bitcast.136), kind=kCustom, calls=%fused_computation.6 | custom fusion | bytes 8192 | tf_op jit(solution)/shard_map/jit(take_along_axis)/gather | solution.py:99
  27.8 5.9 %scatter_fusion = bf16[3584,256]{1,0:T(8,128)(2,1)} fusion(bf16[3584,256]{1,0:T(8,128)(2,1)} %bitcast.141, s32[512]{0:T(512)S(1)} %bitcast.158, bf16[512,256]{1,0:T(8,128)(2,1)S(1)} %copy-done.7), kind=kCustom, calls=%fused_computation.7 | custom fusion | bytes 788480 | tf_op jit(solution)/shard_map/scatter | solution.py:106
  52.0 58.2 %while.20 = (s32[]{:T(128)}, bf16[8,256,2,128]{3,1,2,0:T(8,128)(2,1)S(1)}, s32[1,256]{1,0:T(1,128)S(1)}, bf16[8,256,2,128]{1,3,0,2:T(8,128)(2,1)S(1)}, bf16[1792...) while((s32[]{:T(128)}, bf16[8,256,2,128]{3,1,2,0:T(8,128)(2,1)S(1)}, ...), condition=%wide.region_9.10_spmd, body=%wide.region_6.9_spmd.sunk | while | flops 476710656 | bytes 10818645 | solution.py:126
  52.4 3.7 %fusion.87 = (f32[2,256]{1,0:T(2,128)S(1)}, f32[2,256,1792]{2,1,0:T(8,128)}) fusion(bf16[1792,2,128]{2,0,1:T(8,128)(2,1)S(1)} %get-tuple-element.272, pred[256,1792]{1,0:T(8,128)(4,1)S(1)} %iota_compare_fusion.5, bf16[8,256,2,128]{1,3,0,2:T(8,128)(2,1)S(1)} %get-tuple-element.271, s32[]{:T(128)} %get-tuple-element.261), kind=kOutput, calls=%fused_computation.130.clone.1 | convolution fusion | flops 239470336 | bytes 5638148 | tf_op jit(solution)/shard_map/while/body/eval_jaxpr/sub | solution.py:23
  59.5 3.7 %fusion.87 = (f32[2,256]{1,0:T(2,128)S(1)}, f32[2,256,1792]{2,1,0:T(8,128)}) fusion(bf16[1792,2,128]{2,0,1:T(8,128)(2,1)S(1)} %get-tuple-element.272, pred[256,1792]{1,0:T(8,128)(4,1)S(1)} %iota_compare_fusion.5, bf16[8,256,2,128]{1,3,0,2:T(8,128)(2,1)S(1)} %get-tuple-element.271, s32[]{:T(128)} %get-tuple-element.261), kind=kOutput, calls=%fused_computation.130.clone.1 | convolution fusion | flops 239470336 | bytes 5638148 | tf_op jit(solution)/shard_map/while/body/eval_jaxpr/sub | solution.py:23
  66.6 3.7 %fusion.87 = (f32[2,256]{1,0:T(2,128)S(1)}, f32[2,256,1792]{2,1,0:T(8,128)}) fusion(bf16[1792,2,128]{2,0,1:T(8,128)(2,1)S(1)} %get-tuple-element.272, pred[256,1792]{1,0:T(8,128)(4,1)S(1)} %iota_compare_fusion.5, bf16[8,256,2,128]{1,3,0,2:T(8,128)(2,1)S(1)} %get-tuple-element.271, s32[]{:T(128)} %get-tuple-element.261), kind=kOutput, calls=%fused_computation.130.clone.1 | convolution fusion | flops 239470336 | bytes 5638148 | tf_op jit(solution)/shard_map/while/body/eval_jaxpr/sub | solution.py:23
  73.7 3.7 %fusion.87 = (f32[2,256]{1,0:T(2,128)S(1)}, f32[2,256,1792]{2,1,0:T(8,128)}) fusion(bf16[1792,2,128]{2,0,1:T(8,128)(2,1)S(1)} %get-tuple-element.272, pred[256,1792]{1,0:T(8,128)(4,1)S(1)} %iota_compare_fusion.5, bf16[8,256,2,128]{1,3,0,2:T(8,128)(2,1)S(1)} %get-tuple-element.271, s32[]{:T(128)} %get-tuple-element.261), kind=kOutput, calls=%fused_computation.130.clone.1 | convolution fusion | flops 239470336 | bytes 5638148 | tf_op jit(solution)/shard_map/while/body/eval_jaxpr/sub | solution.py:23
  77.4 4.4 %fusion.88 = bf16[8,256,2,128]{3,1,2,0:T(8,128)(2,1)S(1)} fusion(bf16[8,256,2,128]{3,1,2,0:T(8,128)(2,1)S(1)} %get-tuple-element.262, s32[]{:T(128)} %get-tuple-element.261, bf16[1792,2,128]{2,0,1:T(8,128)(2,1)} %get-tuple-element.273, f32[2,256,1792]{2,1,0:T(8,128)} %get-tuple-element.223, f32[2,256]{1,0:T(2,128)S(1)} %get-tuple-element.224), kind=kOutput, calls=%fused_computation.19.clone.1 | convolution fusion | flops 236781568 | bytes 4720644 | tf_op jit(solution)/shard_map/while/body/eval_jaxpr/kts,skd->tkd/dot_general | solution.py:25
  96.4 3.7 %fusion.87 = (f32[2,256]{1,0:T(2,128)S(1)}, f32[2,256,1792]{2,1,0:T(8,128)}) fusion(bf16[1792,2,128]{2,0,1:T(8,128)(2,1)S(1)} %get-tuple-element.272, pred[256,1792]{1,0:T(8,128)(4,1)S(1)} %iota_compare_fusion.5, bf16[8,256,2,128]{1,3,0,2:T(8,128)(2,1)S(1)} %get-tuple-element.271, s32[]{:T(128)} %get-tuple-element.261), kind=kOutput, calls=%fused_computation.130.clone.1 | convolution fusion | flops 239470336 | bytes 5638148 | tf_op jit(solution)/shard_map/while/body/eval_jaxpr/sub | solution.py:23
  103.5 3.7 %fusion.87 = (f32[2,256]{1,0:T(2,128)S(1)}, f32[2,256,1792]{2,1,0:T(8,128)}) fusion(bf16[1792,2,128]{2,0,1:T(8,128)(2,1)S(1)} %get-tuple-element.272, pred[256,1792]{1,0:T(8,128)(4,1)S(1)} %iota_compare_fusion.5, bf16[8,256,2,128]{1,3,0,2:T(8,128)(2,1)S(1)} %get-tuple-element.271, s32[]{:T(128)} %get-tuple-element.261), kind=kOutput, calls=%fused_computation.130.clone.1 | convolution fusion | flops 239470336 | bytes 5638148 | tf_op jit(solution)/shard_map/while/body/eval_jaxpr/sub | solution.py:23
  118.3 67.2 %while.21 = (s32[]{:T(128)}, bf16[8,256,2,128]{3,1,2,0:T(8,128)(2,1)S(1)}, s32[1,256]{1,0:T(1,128)S(1)}, bf16[8,256,2,128]{1,3,0,2:T(8,128)(2,1)}, bf16[1792,2,1...) while((s32[]{:T(128)}, bf16[8,256,2,128]{3,1,2,0:T(8,128)(2,1)S(1)}, ...), condition=%wide.region_13.14_spmd, body=%wide.region_10.13_spmd.sunk | while | flops 476710656 | bytes 10819153 | solution.py:126
  118.6 5.0 %fusion.92 = (f32[2,256]{1,0:T(2,128)S(1)}, f32[2,256,1792]{2,1,0:T(8,128)}) fusion(bf16[1792,2,128]{2,0,1:T(8,128)(2,1)} %get-tuple-element.251, pred[256,1792]{1,0:T(8,128)(4,1)S(1)} %iota_compare_fusion.6, bf16[8,256,2,128]{1,3,0,2:T(8,128)(2,1)} %get-tuple-element.250, s32[]{:T(128)} %get-tuple-element.240), kind=kOutput, calls=%fused_computation.131.clone.1 | convolution fusion | flops 239470336 | bytes 5638656 | tf_op jit(solution)/shard_map/while/body/eval_jaxpr/sub | solution.py:23
  127.0 5.0 %fusion.92 = (f32[2,256]{1,0:T(2,128)S(1)}, f32[2,256,1792]{2,1,0:T(8,128)}) fusion(bf16[1792,2,128]{2,0,1:T(8,128)(2,1)} %get-tuple-element.251, pred[256,1792]{1,0:T(8,128)(4,1)S(1)} %iota_compare_fusion.6, bf16[8,256,2,128]{1,3,0,2:T(8,128)(2,1)} %get-tuple-element.250, s32[]{:T(128)} %get-tuple-element.240), kind=kOutput, calls=%fused_computation.131.clone.1 | convolution fusion | flops 239470336 | bytes 5638656 | tf_op jit(solution)/shard_map/while/body/eval_jaxpr/sub | solution.py:23
  135.4 5.0 %fusion.92 = (f32[2,256]{1,0:T(2,128)S(1)}, f32[2,256,1792]{2,1,0:T(8,128)}) fusion(bf16[1792,2,128]{2,0,1:T(8,128)(2,1)} %get-tuple-element.251, pred[256,1792]{1,0:T(8,128)(4,1)S(1)} %iota_compare_fusion.6, bf16[8,256,2,128]{1,3,0,2:T(8,128)(2,1)} %get-tuple-element.250, s32[]{:T(128)} %get-tuple-element.240), kind=kOutput, calls=%fused_computation.131.clone.1 | convolution fusion | flops 239470336 | bytes 5638656 | tf_op jit(solution)/shard_map/while/body/eval_jaxpr/sub | solution.py:23
  143.7 5.0 %fusion.92 = (f32[2,256]{1,0:T(2,128)S(1)}, f32[2,256,1792]{2,1,0:T(8,128)}) fusion(bf16[1792,2,128]{2,0,1:T(8,128)(2,1)} %get-tuple-element.251, pred[256,1792]{1,0:T(8,128)(4,1)S(1)} %iota_compare_fusion.6, bf16[8,256,2,128]{1,3,0,2:T(8,128)(2,1)} %get-tuple-element.250, s32[]{:T(128)} %get-tuple-element.240), kind=kOutput, calls=%fused_computation.131.clone.1 | convolution fusion | flops 239470336 | bytes 5638656 | tf_op jit(solution)/shard_map/while/body/eval_jaxpr/sub | solution.py:23
  152.3 5.0 %fusion.92 = (f32[2,256]{1,0:T(2,128)S(1)}, f32[2,256,1792]{2,1,0:T(8,128)}) fusion(bf16[1792,2,128]{2,0,1:T(8,128)(2,1)} %get-tuple-element.251, pred[256,1792]{1,0:T(8,128)(4,1)S(1)} %iota_compare_fusion.6, bf16[8,256,2,128]{1,3,0,2:T(8,128)(2,1)} %get-tuple-element.250, s32[]{:T(128)} %get-tuple-element.240), kind=kOutput, calls=%fused_computation.131.clone.1 | convolution fusion | flops 239470336 | bytes 5638656 | tf_op jit(solution)/shard_map/while/body/eval_jaxpr/sub | solution.py:23
  160.7 5.0 %fusion.92 = (f32[2,256]{1,0:T(2,128)S(1)}, f32[2,256,1792]{2,1,0:T(8,128)}) fusion(bf16[1792,2,128]{2,0,1:T(8,128)(2,1)} %get-tuple-element.251, pred[256,1792]{1,0:T(8,128)(4,1)S(1)} %iota_compare_fusion.6, bf16[8,256,2,128]{1,3,0,2:T(8,128)(2,1)} %get-tuple-element.250, s32[]{:T(128)} %get-tuple-element.240), kind=kOutput, calls=%fused_computation.131.clone.1 | convolution fusion | flops 239470336 | bytes 5638656 | tf_op jit(solution)/shard_map/while/body/eval_jaxpr/sub | solution.py:23
  169.1 5.0 %fusion.92 = (f32[2,256]{1,0:T(2,128)S(1)}, f32[2,256,1792]{2,1,0:T(8,128)}) fusion(bf16[1792,2,128]{2,0,1:T(8,128)(2,1)} %get-tuple-element.251, pred[256,1792]{1,0:T(8,128)(4,1)S(1)} %iota_compare_fusion.6, bf16[8,256,2,128]{1,3,0,2:T(8,128)(2,1)} %get-tuple-element.250, s32[]{:T(128)} %get-tuple-element.240), kind=kOutput, calls=%fused_computation.131.clone.1 | convolution fusion | flops 239470336 | bytes 5638656 | tf_op jit(solution)/shard_map/while/body/eval_jaxpr/sub | solution.py:23
  177.4 5.0 %fusion.92 = (f32[2,256]{1,0:T(2,128)S(1)}, f32[2,256,1792]{2,1,0:T(8,128)}) fusion(bf16[1792,2,128]{2,0,1:T(8,128)(2,1)} %get-tuple-element.251, pred[256,1792]{1,0:T(8,128)(4,1)S(1)} %iota_compare_fusion.6, bf16[8,256,2,128]{1,3,0,2:T(8,128)(2,1)} %get-tuple-element.250, s32[]{:T(128)} %get-tuple-element.240), kind=kOutput, calls=%fused_computation.131.clone.1 | convolution fusion | flops 239470336 | bytes 5638656 | tf_op jit(solution)/shard_map/while/body/eval_jaxpr/sub | solution.py:23
  204.3 26.1 %all-to-all-done = bf16[8,64,2048]{2,1,0:T(8,128)(2,1)S(1)} async-done(((bf16[8,64,2048]{2,1,0:T(8,128)(2,1)}), bf16[8,64,2048]{2,1,0:T(8,128)(2,1)S(1)}, u32[]{:S(2)}, u32[]{:S(2)}) %all-to-all-start) | async-done | bytes 2097184 | tf_op jit(solution)/shard_map/all_to_all | solution.py:50
  230.4 3.8 %scatter_custom_fusion.2 = bf16[264,2048]{1,0:T(8,128)(2,1)S(1)} fusion(s32[512]{0:T(512)S(1)} %bitcast.166, bf16[512,2048]{1,0:T(8,128)(2,1)S(1)} %bitcast.152, bf16[]{:T(256)} %constant.156.clone.1), kind=kCustom, calls=%fused_computation.54 | custom fusion | bytes 1081346 | tf_op jit(solution)/shard_map/scatter | solution.py:56
  234.2 16.5 %convolution_convert_fusion = bf16[264,8192]{1,0:T(8,128)(2,1)} fusion(bf16[264,2048]{1,0:T(8,128)(2,1)S(1)} %scatter_custom_fusion.2, bf16[2048,8192]{1,0:T(8,128)(2,1)} %all-gather.2.cloned.1.call-done), kind=kOutput, calls=%fused_computation.48 | convolution fusion | flops 8860532736 | bytes 38961152 | tf_op jit(solution)/shard_map/dot_general | solution.py:60
  250.8 78.3 %reduce-scatter.2.cloned.1.call-done = bf16[264,2048]{1,0:T(8,128)(2,1)} async-done(((bf16[264,8192]{1,0:T(8,128)(2,1)}), bf16[264,2048]{1,0:T(8,128)(2,1)}) %reduce-scatter.2.cloned.1.call-update) | async-done | bytes 1081360 | tf_op jit(solution)/shard_map/reduce_scatter | solution.py:68
  (136 shorter events, 110.9 us)
Async XLA Ops:
  7.2 227.0 %all-gather.2.cloned.1.call-start = ((), (), s32[]{:S(2)}) async-start(), calls=%async_computation.2 | async-start | bytes 37748736 | tf_op jit(solution)/shard_map/all_gather | solution.py:62
  10.1 0.7 copy-start.11
  10.1 2.0 copy-start.10
  10.1 12.5 %copy-start.9 = (s32[2]{0:T(128)S(1)}, s32[2]{0:T(128)}, u32[]{:S(2)}) copy-start(s32[2]{0:T(128)} %param.22) | copy-start | bytes 28
  10.1 12.8 %copy-start = (s32[2,14]{1,0:T(2,128)S(1)}, s32[2,14]{1,0:T(2,128)}, u32[]{:S(2)}) copy-start(s32[2,14]{1,0:T(2,128)} %param.20) | copy-start | bytes 340
  10.2 17.6 %copy-start.7 = (bf16[512,256]{1,0:T(8,128)(2,1)S(1)}, bf16[512,256]{1,0:T(8,128)(2,1)}, u32[]{:S(2)}) copy-start(bf16[512,256]{1,0:T(8,128)(2,1)} %param.16) | copy-start | bytes 786436
  27.7 8.0 %copy-start.2 = (bf16[28,128,256]{2,1,0:T(8,128)(2,1)S(1)}, bf16[28,128,256]{2,1,0:T(8,128)(2,1)}, u32[]{:S(2)}) copy-start(bf16[28,128,256]{2,1,0:T(8,128)(2,1)} %param.19) | copy-start | bytes 5505028
  27.7 8.0 %copy-start.8 = (bf16[512,256]{1,0:T(8,128)(2,1)S(1)}, bf16[512,256]{1,0:T(8,128)(2,1)}, u32[]{:S(2)}) copy-start(bf16[512,256]{1,0:T(8,128)(2,1)} %param.17) | copy-start | bytes 786436
  39.2 6.2 %copy-start.1 = (bf16[3584,256]{1,0:T(8,128)(2,1)}, bf16[3584,256]{1,0:T(8,128)(2,1)S(1)}, u32[]{:S(2)}) copy-start(bf16[3584,256]{1,0:T(8,128)(2,1)S(1)} %scatter_fusion.1) | copy-start | bytes 5505028
  45.4 2.0 copy-start.5
  111.0 1.2 copy-start.4
  113.4 3.3 copy-start.3
  200.2 30.2 %all-to-all-start = ((bf16[8,64,2048]{2,1,0:T(8,128)(2,1)}), bf16[8,64,2048]{2,1,0:T(8,128)(2,1)S(1)}, u32[]{:S(2)}, u32[]{:S(2)}) async-start(bf16[8,64,2048]{2,1,0:T(8,128)(2,1)} %select_select_fusion), calls=%async_computation | async-start | bytes 4194304 | tf_op jit(solution)/shard_map/all_to_all | solution.py:50
  203.8 125.2 %reduce-scatter.2.cloned.1.call-start = ((), (), s32[]{:S(2)}) async-start(), calls=%async_computation.3 | async-start | bytes 5406720 | tf_op jit(solution)/shard_map/reduce_scatter | solution.py:68
  250.7 78.3 %copy-start.6 = (bf16[264,2048]{1,0:T(8,128)(2,1)S(1)}, bf16[264,2048]{1,0:T(8,128)(2,1)}, u32[]{:S(2)}) copy-start(bf16[264,2048]{1,0:T(8,128)(2,1)} %param.24) | copy-start | bytes 3244036
Sparse Core Ops, SparseCore 0:
  10.3 163.3 all-gather.1
  250.9 78.0 reduce-scatter.1

commit v2 on v1

--- a/solution.py
+++ b/solution.py
@@ -4,6 +4,8 @@
 import jax.numpy as jnp
 from jax import lax
 from jax.sharding import PartitionSpec as P
+from jax.experimental import pallas as pl
+from jax.experimental.pallas import tpu as pltpu
 
 HEAD_SIZE = 128
 
@@ -11,19 +13,55 @@
 NEGATIVE = -1e30
 
 
-def head_attention(query_matrix, prior_keys, prior_values, visible, scale_factor):
-    scores = (
-        jnp.einsum("tkd,skd->kts", query_matrix, prior_keys, preferred_element_type=jnp.float32)
-        * scale_factor
-    )
-    spots_all = jnp.arange(prior_keys.shape[0], dtype=jnp.int32)
-    allowed = spots_all[None, None, :] <= visible[None, :, None]
-    scores = jnp.where(allowed, scores, NEGATIVE)
-    highest = jnp.max(scores, axis=2, keepdims=True)
-    expo_terms = jnp.where(allowed, jnp.exp(scores - highest), 0.0)
-    weights = (expo_terms / jnp.sum(expo_terms, axis=2, keepdims=True)).astype(jnp.bfloat16)
-    mixed = jnp.einsum("kts,skd->tkd", weights, prior_values, preferred_element_type=jnp.float32)
-    return mixed.astype(jnp.bfloat16)
+def attention_kernel(cached_ref, q_ref, k_ref, v_ref, o_ref, *, fanout, scale_factor):
+    member = pl.program_id(0)
+    rows = q_ref.shape[0]
+    spots = k_ref.shape[0]
+    row_ids = lax.broadcasted_iota(jnp.int32, (rows, spots), 0)
+    col_ids = lax.broadcasted_iota(jnp.int32, (rows, spots), 1)
+    allowed = col_ids <= row_ids + cached_ref[member]
+    keys = k_ref[...]
+    values = v_ref[...]
+    for head in range(fanout):
+        lanes = slice(head * HEAD_SIZE, (head + 1) * HEAD_SIZE)
+        scores = (
+            lax.dot_general(
+                q_ref[:, lanes], keys, (((1,), (1,)), ((), ())),
+                preferred_element_type=jnp.float32,
+            )
+            * scale_factor
+        )
+        scores = jnp.where(allowed, scores, NEGATIVE)
+        highest = jnp.max(scores, axis=1, keepdims=True)
+        expo_terms = jnp.exp(scores - highest)
+        weights = (expo_terms / jnp.sum(expo_terms, axis=1, keepdims=True)).astype(jnp.bfloat16)
+        mixed = jnp.dot(weights, values, preferred_element_type=jnp.float32)
+        o_ref[:, lanes] = mixed.astype(o_ref.dtype)
+
+
+def paged_attention(queries, prior_keys, prior_values, cached_lens, fanout, scale_factor):
+    per_group, spots, channel_count = prior_keys.shape
+    kv_local = channel_count // HEAD_SIZE
+    new_limit = queries.shape[0] // per_group
+    width = fanout * HEAD_SIZE
+    kernel = lambda *refs: attention_kernel(*refs, fanout=fanout, scale_factor=scale_factor)
+    return pl.pallas_call(
+        kernel,
+        grid_spec=pltpu.PrefetchScalarGridSpec(
+            num_scalar_prefetch=1,
+            grid=(per_group, kv_local),
+            in_specs=[
+                pl.BlockSpec((new_limit, width), lambda m, g, c: (m, g)),
+                pl.BlockSpec((None, spots, HEAD_SIZE), lambda m, g, c: (m, 0, g)),
+                pl.BlockSpec((None, spots, HEAD_SIZE), lambda m, g, c: (m, 0, g)),
+            ],
+            out_specs=pl.BlockSpec((new_limit, width), lambda m, g, c: (m, g)),
+        ),
+        out_shape=jax.ShapeDtypeStruct(queries.shape, jnp.bfloat16),
+        compiler_params=pltpu.CompilerParams(
+            dimension_semantics=("arbitrary", "arbitrary"),
+        ),
+    )(cached_lens, queries, prior_keys, prior_values)
 
 
 def deal(row_block, new_counts, lead_in, shares, starts, totals, balanced):
@@ -110,25 +148,12 @@
     gathered_keys = flat_keys.reshape(key_page_pool.shape)
     gathered_values = flat_values.reshape(value_page_pool.shape)
     scale_factor = 1.0 / math.sqrt(HEAD_SIZE)
-    pieces = []
-    for member in range(per_group):
-        prior_keys = gathered_keys[page_table[member]].reshape(
-            page_count * page_rows, kv_local, HEAD_SIZE
-        )
-        prior_values = gathered_values[page_table[member]].reshape(
-            page_count * page_rows, kv_local, HEAD_SIZE
-        )
-        query_matrix = queries[member * new_limit : (member + 1) * new_limit].reshape(
-            new_limit, kv_local, group_fanout, HEAD_SIZE
-        )
-        query_matrix = jnp.moveaxis(query_matrix, 2, 0)
-        visible = positions[member]
-        mixed = lax.map(
-            lambda single: head_attention(single, prior_keys, prior_values, visible, scale_factor),
-            query_matrix,
-        )
-        pieces.append(jnp.moveaxis(mixed, 0, 2).reshape(new_limit, q_width))
-    attended = jnp.concatenate(pieces, axis=0)
+    table = page_table
+    prior_keys = gathered_keys[table].reshape(per_group, page_count * page_rows, channel_count)
+    prior_values = gathered_values[table].reshape(per_group, page_count * page_rows, channel_count)
+    attended = paged_attention(
+        queries, prior_keys, prior_values, cached_lens, group_fanout, scale_factor
+    )
     load_counts, offsets_all = (
         lax.all_gather(new_counts, "req", axis=0, tiled=True),
         lax.all_gather(deal_offset, "req", axis=0, tiled=True),

time: 339 us -> 301 us (0.89)
  matrix products: 136 us -> 16.5 us
  waiting for transfers between devices: 104 us -> 175 us
  Pallas kernels: 0 us -> 38.5 us
  local copies, waits for them, and re-layouts: 53.6 us -> 35 us
  other arithmetic: 14.8 us -> 6.52 us
    sub x16 -> x0, matrix products: 69.7 us -> none  [head_attention(): expo_terms = jnp.where(allowed, jnp.exp(scores - highest), 0.0)]
    dot_general x16 -> x0, matrix products: 50.2 us -> none  [head_attention(): jnp.einsum('kts,skd->tkd', weights, prior_values, preferred_element_type=...]
    all_gather x1, waiting for transfers between devices: 0.02 us -> 46.7 us  [project(): lax.all_gather(out_weight, 'req', axis=1, tiled=True)]
    pallas_call x0 -> x1, Pallas kernels: none -> 38.5 us  [paged_attention(): pl.pallas_call(kernel, grid_spec=pltpu.PrefetchScalarGridSpec(num_scalar_...]
    all_to_all x1, waiting for transfers between devices: 26.1 us -> 48.8 us  [deal(): lax.all_to_all(outgoing, 'req', split_axis=0, concat_axis=0, tiled=True)]
    unnamed x42 -> x36, local copies, waits for them, and re-layouts: 8.89 us -> 3.02 us
    le x16 -> x0, other arithmetic: 5.17 us -> none  [head_attention(): allowed = spots_all[None, None, :] <= visible[None, :, None]]
    gather x4 -> x2, local copies, waits for them, and re-layouts: 8.29 us -> 5.51 us  [the longest x1 3.59 us: local(): gathered_keys[table]]
  transfers between devices with their start and end apart: 3 -> 3, of which waited for: 2 -> 3; matrix products, arithmetic and copies ran while one was open for 54% -> 13% of each run, Pallas kernels for 0% -> 13%
where the time goes in v2:
time: 301 us
  waiting for transfers between devices  175 us (58%)
  Pallas kernels  38.5 us (13%)
  local copies, waits for them, and re-layouts  35 us (12%)
  matrix products  16.5 us (5%)
  between operations  15.8 us (5%)
  blocking collectives  9.49 us (3%)
  other arithmetic  6.52 us (2%)
  starting transfers between devices  3.9 us (1%)
    reduce_scatter x1, waiting for transfers between devices, head_total(): lax.psum_scatter(partial_sum.astype(jnp.bfloat16), 'head', scatter_dimens...  79.1 us
    all_to_all x1, waiting for transfers between devices, deal(): lax.all_to_all(outgoing, 'req', split_axis=0, concat_axis=0, tiled=True)  48.8 us
    all_gather x1, waiting for transfers between devices, project(): lax.all_gather(out_weight, 'req', axis=1, tiled=True)  46.7 us
    pallas_call x1, Pallas kernels, paged_attention(): pl.pallas_call(kernel, grid_spec=pltpu.PrefetchScalarGridSpec(num_scalar_...  38.5 us
    dot_general x1, matrix products, project(): jnp.dot(row_block, lax.all_gather(out_weight, 'req', axis=1, tiled=True),...  16.5 us
    unnamed x1, blocking collectives  9.49 us
    gather x1, local copies, waits for them, and re-layouts, deal(): jnp.take(row_block, source.reshape(-1), axis=0)  6.27 us
  transfers between devices with their start and end apart: 3, of which 3 were waited for; matrix products, arithmetic and copies ran while one was open for 13% of the time, Pallas kernels for 13%

profile of v2, /device:TPU:0, one launch (start us, length us, event | category | flops | bytes accessed | tf_op | source)
XLA Modules:
  0.0 300.9 jit_solution(8050157050630059710)
XLA Ops:
  7.3 0.6 all-gather.2.cloned.1.call-update
  8.7 0.6 dynamic-slice
  10.2 0.8 dynamic-update-slice.1
  11.0 9.5 %all-reduce.2 = (s32[16]{0:T(128)S(1)}, s32[8]{0:T(128)S(1)}) all-reduce(s32[16]{0:T(128)S(1)} %dynamic-update-slice, s32[8]{0:T(128)S(1)} %dynamic-update-slice.1), channel_id=1, replica_groups=mesh['req'=8,'head'=4] {'req'}, use_global_device_ids=true, to_apply=%add | all-reduce | flops 24 | bytes 192
  21.0 0.6 dynamic_slice.18
  22.3 4.8 %gather_fusion.4 = s32[512]{0:T(512)S(1)} fusion(s32[2,14]{1,0:T(2,128)S(1)} %copy-done, s32[512]{0:T(512)S(1)} %bitcast.52), kind=kCustom, calls=%fused_computation.4 | custom fusion | bytes 8192 | tf_op jit(solution)/shard_map/jit(take_along_axis)/gather | solution.py:137
  27.3 3.4 %scatter_fusion = bf16[3584,256]{1,0:T(8,128)(2,1)S(1)} fusion(bf16[3584,256]{1,0:T(8,128)(2,1)S(1)} %bitcast.58, s32[512]{0:T(512)S(1)} %bitcast.64, bf16[512,256]{1,0:T(8,128)(2,1)S(1)} %copy-done.6), kind=kCustom, calls=%fused_computation.5 | custom fusion | bytes 788480 | tf_op jit(solution)/shard_map/scatter | solution.py:144
  30.7 1.2 copy-done.3
  31.9 3.6 %gather_fusion.1 = bf16[28,128,256]{2,1,0:T(8,128)(2,1)} fusion(bf16[28,128,256]{2,1,0:T(8,128)(2,1)} %bitcast.56, s32[1024]{0:T(1024)S(1)} %pad_clamp_fusion.1), kind=kCustom, calls=%fused_computation.1 | custom fusion | bytes 3670128 | tf_op jit(solution)/shard_map/gather | solution.py:152
  35.5 3.6 %scatter_fusion.1 = bf16[3584,256]{1,0:T(8,128)(2,1)S(1)} fusion(bf16[3584,256]{1,0:T(8,128)(2,1)S(1)} %bitcast.55, s32[512]{0:T(512)S(1)} %bitcast.65, bf16[512,256]{1,0:T(8,128)(2,1)S(1)} %copy-done.7), kind=kCustom, calls=%fused_computation.6 | custom fusion | bytes 788480 | tf_op jit(solution)/shard_map/scatter | solution.py:146
  39.1 1.9 gather_fusion.2
  41.0 3.3 %gather_fusion = s32[512]{0:T(512)S(1)} fusion(s32[2]{0:T(128)S(1)} %bitcast_subtract_fusion, s32[1024]{0:T(1024)S(1)} %pad_clamp_fusion.2), kind=kCustom, calls=%fused_computation | custom fusion | bytes 6144 | tf_op jit(solution)/shard_map/jit(_take)/gather | solution.py:82
  44.4 38.5 %shard_map.130 = bf16[512,2048]{1,0:T(8,128)(2,1)} custom-call(s32[2]{0:T(128)} %refs_0_.1, bf16[512,2048]{1,0:T(8,128)(2,1)} %refs_1_.1, bf16[2,1792,256]{2,1,0:T(8,128)(2,1)} %bitcast.60, bf16[2,1792,256]{2,1,0:T(8,128)(2,1)} %bitcast.61), custom_call_target="tpu_custom_call" | custom-call | tf_op jit(solution)/shard_map/pallas_call | solution.py:48
  82.9 0.7 compare_select_fusion
  83.6 6.3 %gather_fusion.3 = bf16[512,2048]{1,0:T(8,128)(2,1)S(1)} fusion(bf16[512,2048]{1,0:T(8,128)(2,1)} %shard_map.130, s32[1024]{0:T(1024)S(1)} %pad_clamp_fusion), kind=kCustom, calls=%fused_computation.3 | custom fusion | bytes 4196352 | tf_op jit(solution)/shard_map/jit(_take)/gather | solution.py:86
  89.9 0.7 add_compare_fusion
  90.6 1.6 select_select_fusion
  92.2 3.6 %all-to-all-start = ((bf16[8,64,2048]{2,1,0:T(8,128)(2,1)}), bf16[8,64,2048]{2,1,0:T(8,128)(2,1)S(1)}, u32[]{:S(2)}, u32[]{:S(2)}) async-start(bf16[8,64,2048]{2,1,0:T(8,128)(2,1)} %select_select_fusion), calls=%async_computation | async-start | bytes 4194304 | tf_op jit(solution)/shard_map/all_to_all | solution.py:88
  96.5 48.8 %all-to-all-done = bf16[8,64,2048]{2,1,0:T(8,128)(2,1)S(1)} async-done(((bf16[8,64,2048]{2,1,0:T(8,128)(2,1)}), bf16[8,64,2048]{2,1,0:T(8,128)(2,1)S(1)}, u32[]{:S(2)}, u32[]{:S(2)}) %all-to-all-start) | async-done | bytes 2097184 | tf_op jit(solution)/shard_map/all_to_all | solution.py:88
  145.2 3.8 %scatter_custom_fusion.2 = bf16[264,2048]{1,0:T(8,128)(2,1)S(1)} fusion(s32[512]{0:T(512)S(1)} %bitcast.72, bf16[512,2048]{1,0:T(8,128)(2,1)S(1)} %bitcast.62, bf16[]{:T(256)} %constant.123.clone.1), kind=kCustom, calls=%fused_computation.11 | custom fusion | bytes 1081346 | tf_op jit(solution)/shard_map/scatter | solution.py:94
  149.0 46.7 %all-gather.2.cloned.1.call-done = bf16[2048,8192]{1,0:T(8,128)(2,1)} async-done(((bf16[2048,1024]{1,0:T(8,128)(2,1)}), bf16[2048,8192]{1,0:T(8,128)(2,1)}) %all-gather.2.cloned.1.call-update) | async-done | bytes 33554448 | tf_op jit(solution)/shard_map/all_gather | solution.py:100
  195.8 16.5 %convolution_convert_fusion = bf16[264,8192]{1,0:T(8,128)(2,1)} fusion(bf16[264,2048]{1,0:T(8,128)(2,1)S(1)} %scatter_custom_fusion.2, bf16[2048,8192]{1,0:T(8,128)(2,1)} %all-gather.2.cloned.1.call-done), kind=kOutput, calls=%fused_computation.8 | convolution fusion | flops 8860532736 | bytes 38961152 | tf_op jit(solution)/shard_map/dot_general | solution.py:98
  212.3 79.1 %reduce-scatter.2.cloned.1.call-done = bf16[264,2048]{1,0:T(8,128)(2,1)} async-done(((bf16[264,8192]{1,0:T(8,128)(2,1)}), bf16[264,2048]{1,0:T(8,128)(2,1)}) %reduce-scatter.2.cloned.1.call-update) | async-done | bytes 1081360 | tf_op jit(solution)/shard_map/reduce_scatter | solution.py:106
  291.4 2.6 add_convert_fusion
  (64 shorter events, 2.4 us)
Async XLA Ops:
  7.2 188.6 %all-gather.2.cloned.1.call-start = ((), (), s32[]{:S(2)}) async-start(), calls=%async_computation.2 | async-start | bytes 37748736 | tf_op jit(solution)/shard_map/all_gather | solution.py:100
  7.2 1.5 copy-start.10
  7.2 2.8 copy-start.9
  7.2 14.8 %copy-start.8 = (s32[2]{0:T(128)S(1)}, s32[2]{0:T(128)}, u32[]{:S(2)}) copy-start(s32[2]{0:T(128)} %refs_0_.1) | copy-start | bytes 28
  7.2 15.1 %copy-start = (s32[2,14]{1,0:T(2,128)S(1)}, s32[2,14]{1,0:T(2,128)}, u32[]{:S(2)}) copy-start(s32[2,14]{1,0:T(2,128)} %param.16) | copy-start | bytes 340
  7.9 19.3 %copy-start.4 = (bf16[28,128,256]{2,1,0:T(8,128)(2,1)S(1)}, bf16[28,128,256]{2,1,0:T(8,128)(2,1)}, u32[]{:S(2)}) copy-start(bf16[28,128,256]{2,1,0:T(8,128)(2,1)} %param.14) | copy-start | bytes 5505028
  7.9 19.3 %copy-start.6 = (bf16[512,256]{1,0:T(8,128)(2,1)S(1)}, bf16[512,256]{1,0:T(8,128)(2,1)}, u32[]{:S(2)}) copy-start(bf16[512,256]{1,0:T(8,128)(2,1)} %param.12) | copy-start | bytes 786436
  30.6 1.2 copy-start.3
  31.9 3.6 %copy-start.2 = (bf16[28,128,256]{2,1,0:T(8,128)(2,1)S(1)}, bf16[28,128,256]{2,1,0:T(8,128)(2,1)}, u32[]{:S(2)}) copy-start(bf16[28,128,256]{2,1,0:T(8,128)(2,1)} %param.15) | copy-start | bytes 5505028
  31.9 3.6 %copy-start.7 = (bf16[512,256]{1,0:T(8,128)(2,1)S(1)}, bf16[512,256]{1,0:T(8,128)(2,1)}, u32[]{:S(2)}) copy-start(bf16[512,256]{1,0:T(8,128)(2,1)} %param.13) | copy-start | bytes 786436
  39.0 1.9 copy-start.1
  92.2 53.0 %all-to-all-start = ((bf16[8,64,2048]{2,1,0:T(8,128)(2,1)}), bf16[8,64,2048]{2,1,0:T(8,128)(2,1)S(1)}, u32[]{:S(2)}, u32[]{:S(2)}) async-start(bf16[8,64,2048]{2,1,0:T(8,128)(2,1)} %select_select_fusion), calls=%async_computation | async-start | bytes 4194304 | tf_op jit(solution)/shard_map/all_to_all | solution.py:88
  95.8 195.6 %reduce-scatter.2.cloned.1.call-start = ((), (), s32[]{:S(2)}) async-start(), calls=%async_computation.3 | async-start | bytes 5406720 | tf_op jit(solution)/shard_map/reduce_scatter | solution.py:106
  212.3 79.1 %copy-start.5 = (bf16[264,2048]{1,0:T(8,128)(2,1)S(1)}, bf16[264,2048]{1,0:T(8,128)(2,1)}, u32[]{:S(2)}) copy-start(bf16[264,2048]{1,0:T(8,128)(2,1)} %param.20) | copy-start | bytes 3244036
Sparse Core Ops, SparseCore 0:
  9.9 185.8 all-gather.1
  212.4 78.9 reduce-scatter.1

commit v3 on v2

--- a/solution.py
+++ b/solution.py
@@ -94,18 +94,42 @@
     return blank_rows.at[landing.reshape(-1)].set(arrived.reshape(-1, columns), mode="drop")
 
 
-def project(row_block, out_weight):
-    return jnp.dot(
-        row_block,
-        lax.all_gather(out_weight, "req", axis=1, tiled=True),
-        preferred_element_type=jnp.float32,
-    )
-
-
-def head_total(partial_sum):
-    return lax.psum_scatter(
-        partial_sum.astype(jnp.bfloat16), "head", scatter_dimension=1, tiled=True
-    ).astype(jnp.float32)
+def paired_rows(block, partner, first):
+    return jnp.where(first, jnp.concatenate([block, partner]), jnp.concatenate([partner, block]))
+
+
+def project_and_sum(row_block, out_weight):
+    groups = lax.axis_size("req")
+    head_groups = lax.axis_size("head")
+    my_rank = lax.axis_index("req")
+    is_first = my_rank % 2 == 0
+    pair_perm = [(i, i ^ 1) for i in range(groups)]
+    half = groups // 2
+    weight_blocks = [out_weight]
+    for step in range(1, half):
+        weight_blocks.append(
+            lax.ppermute(out_weight, "req", [(i, i ^ (2 * step)) for i in range(groups)])
+        )
+    order = jnp.arange(half, dtype=jnp.int32) ^ (my_rank // 2)
+    weight_sorted = jnp.take(jnp.stack(weight_blocks), order, axis=0)
+    inner, block_cols = out_weight.shape
+    weight_sorted = jnp.moveaxis(weight_sorted, 0, 1).reshape(inner, half * block_cols)
+    rows = row_block.shape[0]
+    both_rows = paired_rows(row_block, lax.ppermute(row_block, "req", pair_perm), is_first)
+    partial_sum = jnp.dot(both_rows, weight_sorted, preferred_element_type=jnp.float32)
+    per_chunk = half // head_groups
+    partial_sum = partial_sum.astype(jnp.bfloat16).reshape(2 * rows, head_groups, per_chunk * block_cols)
+    reduced = lax.psum_scatter(
+        jnp.moveaxis(partial_sum, 1, 0), "head", scatter_dimension=0, tiled=True
+    )[0]
+    own_rows = jnp.where(is_first, reduced[:rows], reduced[rows:])
+    other_rows = jnp.where(is_first, reduced[rows:], reduced[:rows])
+    arrived = lax.ppermute(other_rows, "req", pair_perm)
+    mine = own_rows.reshape(rows, per_chunk, block_cols)
+    theirs = arrived.reshape(rows, per_chunk, block_cols)
+    even = jnp.where(is_first, mine, theirs)
+    odd = jnp.where(is_first, theirs, mine)
+    return jnp.stack([even, odd], axis=2).reshape(rows, 2 * per_chunk * block_cols)
 
 
 def local(
@@ -164,7 +188,7 @@
     shares = jnp.maximum((totals[:, None] - lead_in + groups - 1) // groups, 0)
     starts = jnp.cumsum(shares, axis=0) - shares
     placed = deal(attended, new_counts, lead_in, shares, starts, totals, balanced)
-    summed = head_total(project(placed, out_weight)).astype(jnp.bfloat16)
+    summed = project_and_sum(placed, out_weight)
     hidden = (residual.astype(jnp.float32) + summed.astype(jnp.float32)).astype(jnp.bfloat16)
     return (hidden, gathered_keys, gathered_values)
 

time: 301 us -> 491 us (1.63)
  blocking collectives: 9.49 us -> 179 us
  waiting for transfers between devices: 175 us -> 106 us
  local copies, waits for them, and re-layouts: 35 us -> 89.5 us
  other arithmetic: 6.52 us -> 35.4 us
  starting transfers between devices: 3.9 us -> 8.82 us
    unnamed x1, blocking collectives: 9.49 us -> 179 us
    all_gather x1 -> x0, waiting for transfers between devices: 46.7 us -> none  [project(): lax.all_gather(out_weight, 'req', axis=1, tiled=True)]
    gather x0 -> x4, local copies, waits for them, and re-layouts: none -> 22.9 us  [project_and_sum(): weight_sorted = jnp.take(jnp.stack(weight_blocks), order, axis=0)]
    all_to_all x1, waiting for transfers between devices: 48.8 us -> 25.9 us  [deal(): lax.all_to_all(outgoing, 'req', split_axis=0, concat_axis=0, tiled=True)]
    select_n x0 -> x1, local copies, waits for them, and re-layouts: none -> 21.9 us  [project_and_sum(): weight_sorted = jnp.take(jnp.stack(weight_blocks), order, axis=0)]
    select_n x0 -> x3, other arithmetic: none -> 16.5 us  [the longest x2 15.3 us: project_and_sum(): weight_sorted = jnp.take(jnp.stack(weight_blocks), order, axis=0)]
    another operation x1 -> x3, other arithmetic: 0.17 us -> 9.68 us  [the longest x1 8.2 us: project_and_sum(): weight_sorted = jnp.take(jnp.stack(weight_blocks), order, axis=0)]
  transfers between devices with their start and end apart: 3 -> 7, of which waited for: 3 -> 3; matrix products, arithmetic and copies ran while one was open for 13% -> 23% of each run, Pallas kernels for 13% -> 8%
where the time goes in v3:
time: 491 us; the launch traced here: 490 us
  blocking collectives  179 us (36%)
  waiting for transfers between devices  106 us (22%)
  local copies, waits for them, and re-layouts  89.5 us (18%)
  Pallas kernels  38.4 us (8%)
  other arithmetic  35.4 us (7%)
  matrix products  16.4 us (3%)
  between operations  15.7 us (3%)
  starting transfers between devices  8.82 us (2%)
    unnamed x1, blocking collectives  179 us
    reduce_scatter x1, waiting for transfers between devices, project_and_sum(): lax.psum_scatter(jnp.moveaxis(partial_sum, 1, 0), 'head', scatter_dimensi...  78.5 us
    pallas_call x1, Pallas kernels, paged_attention(): pl.pallas_call(kernel, grid_spec=pltpu.PrefetchScalarGridSpec(num_scalar_...  38.4 us
    all_to_all x1, waiting for transfers between devices, deal(): lax.all_to_all(outgoing, 'req', split_axis=0, concat_axis=0, tiled=True)  25.9 us
    gather x4, local copies, waits for them, and re-layouts, project_and_sum(): weight_sorted = jnp.take(jnp.stack(weight_blocks), order, axis=0)  22.9 us
    select_n x1, local copies, waits for them, and re-layouts, project_and_sum(): weight_sorted = jnp.take(jnp.stack(weight_blocks), order, axis=0)  21.9 us
    dot_general x1, matrix products, project_and_sum(): jnp.dot(both_rows, weight_sorted, preferred_element_type=jnp.float32)  16.4 us
    select_n x2, other arithmetic, project_and_sum(): weight_sorted = jnp.take(jnp.stack(weight_blocks), order, axis=0)  15.3 us
  transfers between devices with their start and end apart: 7, of which 3 were waited for; matrix products, arithmetic and copies ran while one was open for 23% of the time, Pallas kernels for 8%

profile of v3, /device:TPU:0, one launch (start us, length us, event | category | flops | bytes accessed | tf_op | source)
XLA Modules:
  0.0 489.8 jit_solution(3361073685255348927)
XLA Ops:
  7.2 3.0 copy.42
  10.2 3.9 collective-permute-start.3
  17.8 179.3 %all-reduce.2 = (s32[16]{0:T(128)S(1)}, s32[8]{0:T(128)S(1)}) all-reduce(s32[16]{0:T(128)S(1)} %dynamic-update-slice, s32[8]{0:T(128)S(1)} %dynamic-update-slice.1), channel_id=1, replica_groups=mesh['req'=8,'head'=4] {'req'}, use_global_device_ids=true, to_apply=%add | all-reduce | flops 24 | bytes 192
  197.6 4.8 gather_fusion.4
  202.5 5.5 %scatter_fusion = bf16[3584,256]{1,0:T(8,128)(2,1)} fusion(bf16[3584,256]{1,0:T(8,128)(2,1)} %bitcast.88, s32[512]{0:T(512)S(1)} %bitcast.101, bf16[512,256]{1,0:T(8,128)(2,1)S(1)} %copy-done.5), kind=kCustom, calls=%fused_computation.8 | custom fusion | bytes 788480 | tf_op jit(solution)/shard_map/scatter | solution.py:168
  208.0 3.4 gather_fusion.1
  211.5 3.6 scatter_fusion.1
  218.1 3.3 gather_fusion
  221.6 38.4 %shard_map.130 = bf16[512,2048]{1,0:T(8,128)(2,1)} custom-call(s32[2]{0:T(128)} %refs_0_.1, bf16[512,2048]{1,0:T(8,128)(2,1)} %refs_1_.1, bf16[2,1792,256]{2,1,0:T(8,128)(2,1)} %bitcast.96, bf16[2,1792,256]{2,1,0:T(8,128)(2,1)} %bitcast.97), custom_call_target="tpu_custom_call" | custom-call | tf_op jit(solution)/shard_map/pallas_call | solution.py:48
  260.7 6.3 %gather_fusion.3 = bf16[512,2048]{1,0:T(8,128)(2,1)S(1)} fusion(bf16[512,2048]{1,0:T(8,128)(2,1)} %shard_map.130, s32[1024]{0:T(1024)S(1)} %pad_clamp_fusion.1), kind=kCustom, calls=%fused_computation.3 | custom fusion | bytes 4196352 | tf_op jit(solution)/shard_map/jit(_take)/gather | solution.py:86
  269.4 3.9 all-to-all-start
  274.0 25.9 %all-to-all-done = bf16[8,64,2048]{2,1,0:T(8,128)(2,1)S(1)} async-done(((bf16[8,64,2048]{2,1,0:T(8,128)(2,1)}), bf16[8,64,2048]{2,1,0:T(8,128)(2,1)S(1)}, u32[]{:S(2)}, u32[]{:S(2)}) %all-to-all-start) | async-done | bytes 2097184 | tf_op jit(solution)/shard_map/all_to_all | solution.py:88
  299.9 3.8 scatter_custom_fusion.2
  303.9 3.9 pad_maximum_fusion.1
  307.8 8.2 %pad_maximum_fusion = bf16[4,2048,1024]{2,1,0:T(8,128)(2,1)S(1)} fusion(bf16[1,2048,1024]{2,1,0:T(8,128)(2,1)} %bitcast.23, bf16[1,2048,1024]{2,1,0:T(8,128)(2,1)} %bitcast.22, bf16[1,2048,1024]{2,1,0:T(8,128)(2,1)} %bitcast.21, bf16[1,2048,1024]{2,1,0:T(8,128)(2,1)} %bitcast.20), kind=kLoop, calls=%fused_computation.11 | loop fusion | flops 25165824 | bytes 33554432 | tf_op jit(solution)/shard_map/stack | solution.py:114
  316.0 5.2 %fusion.29 = (bf16[4,768,1024]{2,1,0:T(8,128)(2,1)}, bf16[4,768,1024]{2,1,0:T(8,128)(2,1)}) fusion(bf16[4,2048,1024]{2,1,0:T(8,128)(2,1)S(1)} %pad_maximum_fusion), kind=kLoop, calls=%fused_computation.110 | loop fusion | bytes 25165824 | tf_op jit(solution)/shard_map/jit(_take)/gather | solution.py:114
  321.2 4.9 %gather_fusion.7 = bf16[4,512,1024]{2,1,0:T(8,128)(2,1)} fusion(bf16[4,512,1024]{2,1,0:T(8,128)(2,1)} %pad_maximum_fusion.1, s32[1024]{0:T(1024)S(1)} %pad_clamp_fusion), kind=kCustom, calls=%fused_computation.7 | custom fusion | bytes 8388624 | tf_op jit(solution)/shard_map/jit(_take)/gather | solution.py:114
  326.1 6.4 %gather_fusion.6 = bf16[4,768,1024]{2,1,0:T(8,128)(2,1)} fusion(bf16[4,768,1024]{2,1,0:T(8,128)(2,1)} %get-tuple-element.6, s32[1024]{0:T(1024)S(1)} %pad_clamp_fusion), kind=kCustom, calls=%fused_computation.6 | custom fusion | bytes 12582928 | tf_op jit(solution)/shard_map/jit(_take)/gather | solution.py:114
  332.5 6.4 %gather_fusion.5 = bf16[4,768,1024]{2,1,0:T(8,128)(2,1)} fusion(bf16[4,768,1024]{2,1,0:T(8,128)(2,1)} %get-tuple-element.5, s32[1024]{0:T(1024)S(1)} %pad_clamp_fusion), kind=kCustom, calls=%fused_computation.5 | custom fusion | bytes 12582928 | tf_op jit(solution)/shard_map/jit(_take)/gather | solution.py:114
  338.9 15.3 %fusion = bf16[2048,4,1024]{2,0,1:T(8,128)(2,1)} fusion(bf16[4,512,1024]{2,1,0:T(8,128)(2,1)} %gather_fusion.7, bf16[4,768,1024]{2,1,0:T(8,128)(2,1)} %gather_fusion.6, bf16[4,768,1024]{2,1,0:T(8,128)(2,1)} %gather_fusion.5, pred[4]{0:T(512)(128)(4,1)S(1)} %compare_and_fusion.1), kind=kLoop, calls=%fused_computation.13 | loop fusion | flops 58720256 | bytes 33554436 | tf_op jit(solution)/shard_map/jit(_take)/select_n | solution.py:114
  354.2 21.9 %copy.23 = bf16[2048,4,1024]{0,2,1:T(8,128)(2,1)} copy(bf16[2048,4,1024]{2,0,1:T(8,128)(2,1)} %fusion) | data formatting | bytes 33554432 | tf_op jit(solution)/shard_map/jit(_take)/select_n | solution.py:114
  377.0 16.4 %convolution_convert_fusion = bf16[528,4096]{1,0:T(8,128)(2,1)S(1)} fusion(bf16[2048,4096]{0,1:T(8,128)(2,1)} %bitcast.92, bf16[264,2048]{1,0:T(8,128)(2,1)} %copy-done.9, bf16[264,2048]{1,0:T(8,128)(2,1)} %copy-done.3, pred[]{:T(512)S(6)} %eq.9), kind=kOutput, calls=%fused_computation.14 | convolution fusion | flops 8870264832 | bytes 23265280 | tf_op jit(solution)/shard_map/dot_general | solution.py:119
  393.4 2.5 copy.34
  395.9 78.5 %reduce-scatter.2.cloned.1.call-done = bf16[1,528,1024]{2,1,0:T(8,128)(2,1)} async-done(((bf16[4,528,1024]{2,1,0:T(8,128)(2,1)}), bf16[1,528,1024]{2,1,0:T(8,128)(2,1)}) %reduce-scatter.2.cloned.1.call-update) | async-done | bytes 1081360 | tf_op jit(solution)/shard_map/reduce_scatter | solution.py:122
  (89 shorter events, 19.6 us)
Async XLA Ops:
  7.2 8.4 %copy-start.10 = (u32[32]{0:T(128)S(1)}, u32[32]{0:T(128)}, u32[]{:S(2)}) copy-start(u32[32]{0:T(128)} %constant.199) | copy-start | bytes 388
  7.2 195.4 %copy-start.5 = (bf16[512,256]{1,0:T(8,128)(2,1)S(1)}, bf16[512,256]{1,0:T(8,128)(2,1)}, u32[]{:S(2)}) copy-start(bf16[512,256]{1,0:T(8,128)(2,1)} %param.12) | copy-start | bytes 786436
  7.2 190.4 %copy-start = (s32[2,14]{1,0:T(2,128)S(1)}, s32[2,14]{1,0:T(2,128)}, u32[]{:S(2)}) copy-start(s32[2,14]{1,0:T(2,128)} %param.16) | copy-start | bytes 340
  7.2 8.3 %copy-start.8 = (s32[2]{0:T(128)S(1)}, s32[2]{0:T(128)}, u32[]{:S(2)}) copy-start(s32[2]{0:T(128)} %param.17) | copy-start | bytes 28
  7.2 7.5 %copy-start.7 = (s32[2]{0:T(128)S(1)}, s32[2]{0:T(128)}, u32[]{:S(2)}) copy-start(s32[2]{0:T(128)} %refs_0_.1) | copy-start | bytes 28
  10.2 293.6 %collective-permute-start.3 = (bf16[2048,1024]{1,0:T(8,128)(2,1)}, bf16[2048,1024]{1,0:T(8,128)(2,1)}, u32[]{:S(2)}, u32[]{:S(2)}) collective-permute-start(bf16[2048,1024]{1,0:T(8,128)(2,1)} %param.21), channel_id=1, source_target_pairs={{0,24},{4,28},{8,16},{12,20},{16,8},{20,12},{24,0},{28,4},{1,25},{... | collective-permute-start | bytes 12582920 | tf_op jit(solution)/shard_map/ppermute | solution.py:111
  14.1 289.7 %collective-permute-start.2 = (bf16[2048,1024]{1,0:T(8,128)(2,1)}, bf16[2048,1024]{1,0:T(8,128)(2,1)}, u32[]{:S(2)}, u32[]{:S(2)}) collective-permute-start(bf16[2048,1024]{1,0:T(8,128)(2,1)} %param.21), channel_id=1, source_target_pairs={{0,16},{4,20},{8,24},{12,28},{16,0},{20,4},{24,8},{28,12},{1,17},{... | collective-permute-start | bytes 12582920 | tf_op jit(solution)/shard_map/ppermute | solution.py:111
  14.6 289.2 %collective-permute-start.1 = (bf16[2048,1024]{1,0:T(8,128)(2,1)}, bf16[2048,1024]{1,0:T(8,128)(2,1)}, u32[]{:S(2)}, u32[]{:S(2)}) collective-permute-start(bf16[2048,1024]{1,0:T(8,128)(2,1)} %param.21), channel_id=1, source_target_pairs={{0,8},{4,12},{8,0},{12,4},{16,24},{20,28},{24,16},{28,20},{1,9},{5... | collective-permute-start | bytes 12582920 | tf_op jit(solution)/shard_map/ppermute | solution.py:111
  202.3 9.1 %copy-start.2 = (bf16[28,128,256]{2,1,0:T(8,128)(2,1)S(1)}, bf16[28,128,256]{2,1,0:T(8,128)(2,1)}, u32[]{:S(2)}) copy-start(bf16[28,128,256]{2,1,0:T(8,128)(2,1)} %param.15) | copy-start | bytes 5505028
  202.4 9.1 %copy-start.6 = (bf16[512,256]{1,0:T(8,128)(2,1)S(1)}, bf16[512,256]{1,0:T(8,128)(2,1)}, u32[]{:S(2)}) copy-start(bf16[512,256]{1,0:T(8,128)(2,1)} %param.13) | copy-start | bytes 786436
  215.0 45.0 %copy-start.1 = (bf16[3584,256]{1,0:T(8,128)(2,1)}, bf16[3584,256]{1,0:T(8,128)(2,1)S(1)}, u32[]{:S(2)}) copy-start(bf16[3584,256]{1,0:T(8,128)(2,1)S(1)} %scatter_fusion.1) | copy-start | bytes 5505028
  269.4 30.5 %all-to-all-start = ((bf16[8,64,2048]{2,1,0:T(8,128)(2,1)}), bf16[8,64,2048]{2,1,0:T(8,128)(2,1)S(1)}, u32[]{:S(2)}, u32[]{:S(2)}) async-start(bf16[8,64,2048]{2,1,0:T(8,128)(2,1)} %select_select_fusion), calls=%async_computation | async-start | bytes 4194304 | tf_op jit(solution)/shard_map/all_to_all | solution.py:88
  273.3 201.0 %reduce-scatter.2.cloned.1.call-start = ((), (), s32[]{:S(2)}) async-start(), calls=%async_computation.2 | async-start | bytes 5406720 | tf_op jit(solution)/shard_map/reduce_scatter | solution.py:122
  303.7 4.0 copy-start.3
  303.7 72.3 %collective-permute-start = (bf16[264,2048]{1,0:T(8,128)(2,1)S(1)}, bf16[264,2048]{1,0:T(8,128)(2,1)S(1)}, u32[]{:S(2)}, u32[]{:S(2)}) collective-permute-start(bf16[264,2048]{1,0:T(8,128)(2,1)S(1)} %scatter_custom_fusion.2), channel_id=1, source_target_pairs={{0,4},{4,0},{8,12},{12,8},{16,20},{20,16},{24,28},{28,24},{1,5},{5... | collective-permute-start | bytes 3244040 | tf_op jit(solution)/shard_map/ppermute | solution.py:118
  376.0 1.0 copy-start.9
  475.6 2.0 collective-permute-start.4
  479.0 2.6 copy-start.4
Sparse Core Ops, SparseCore 0:
  396.0 78.2 reduce-scatter.1

commit v4 on v2

--- a/solution.py
+++ b/solution.py
@@ -3,7 +3,7 @@
 import jax
 import jax.numpy as jnp
 from jax import lax
-from jax.sharding import PartitionSpec as P
+from jax.sharding import Mesh, PartitionSpec as P
 from jax.experimental import pallas as pl
 from jax.experimental.pallas import tpu as pltpu
 
@@ -11,6 +11,7 @@
 
 
 NEGATIVE = -1e30
+REQ = ("chip", "core")
 
 
 def attention_kernel(cached_ref, q_ref, k_ref, v_ref, o_ref, *, fanout, scale_factor):
@@ -65,8 +66,8 @@
 
 
 def deal(row_block, new_counts, lead_in, shares, starts, totals, balanced):
-    groups = lax.axis_size("req")
-    my_rank = lax.axis_index("req")
+    groups = lax.axis_size(REQ)
+    my_rank = lax.axis_index(REQ)
     per_group = new_counts.shape[0]
     new_limit = row_block.shape[0] // per_group
     pair_slots = row_block.shape[0] // groups
@@ -85,7 +86,7 @@
     source = jnp.where(is_live, source, 0)
     picked = jnp.take(row_block, source.reshape(-1), axis=0).reshape(groups, pair_slots, columns)
     outgoing = jnp.where(is_live[:, :, None], picked, jnp.zeros((), row_block.dtype))
-    arrived = lax.all_to_all(outgoing, "req", split_axis=0, concat_axis=0, tiled=True)
+    arrived = lax.all_to_all(outgoing, REQ, split_axis=0, concat_axis=0, tiled=True)
     own_shares = lax.dynamic_index_in_dim(shares, my_rank, 1, keepdims=False)
     own_starts = lax.dynamic_index_in_dim(starts, my_rank, 1, keepdims=False)
     within = jnp.arange(pair_slots, dtype=jnp.int32)[None, :]
@@ -94,18 +95,21 @@
     return blank_rows.at[landing.reshape(-1)].set(arrived.reshape(-1, columns), mode="drop")
 
 
-def project(row_block, out_weight):
-    return jnp.dot(
-        row_block,
-        lax.all_gather(out_weight, "req", axis=1, tiled=True),
-        preferred_element_type=jnp.float32,
-    )
-
-
-def head_total(partial_sum):
-    return lax.psum_scatter(
-        partial_sum.astype(jnp.bfloat16), "head", scatter_dimension=1, tiled=True
-    ).astype(jnp.float32)
+def project_and_sum(row_block, out_weight):
+    head_groups = lax.axis_size("head")
+    chips = lax.axis_size("chip")
+    rows = row_block.shape[0]
+    inner, block_cols = out_weight.shape
+    weight_part = lax.all_gather(out_weight, "chip", axis=1, tiled=True)
+    both_rows = lax.all_gather(row_block, "core", axis=0, tiled=True)
+    partial_sum = jnp.dot(both_rows, weight_part, preferred_element_type=jnp.float32)
+    per_chunk = chips // head_groups
+    partial_sum = partial_sum.astype(jnp.bfloat16).reshape(2 * rows, head_groups, per_chunk * block_cols)
+    reduced = lax.psum_scatter(
+        jnp.moveaxis(partial_sum, 1, 0), "head", scatter_dimension=0, tiled=True
+    ).reshape(2, rows, per_chunk, block_cols)
+    arrived = lax.all_to_all(reduced, "core", split_axis=0, concat_axis=0, tiled=True)
+    return jnp.moveaxis(arrived, 0, 2).reshape(rows, 2 * per_chunk * block_cols)
 
 
 def local(
@@ -121,7 +125,7 @@
     residual,
     out_weight,
 ):
-    groups = lax.axis_size("req")
+    groups = lax.axis_size(REQ)
     per_group = new_counts.shape[0]
     page_count = page_table.shape[1]
     page_rows = key_page_pool.shape[1]
@@ -155,8 +159,8 @@
         queries, prior_keys, prior_values, cached_lens, group_fanout, scale_factor
     )
     load_counts, offsets_all = (
-        lax.all_gather(new_counts, "req", axis=0, tiled=True),
-        lax.all_gather(deal_offset, "req", axis=0, tiled=True),
+        lax.all_gather(new_counts, REQ, axis=0, tiled=True),
+        lax.all_gather(deal_offset, REQ, axis=0, tiled=True),
     )
     totals = jnp.sum(load_counts.reshape(groups, per_group), axis=1)
     rank_ids = jnp.arange(groups, dtype=jnp.int32)
@@ -164,29 +168,33 @@
     shares = jnp.maximum((totals[:, None] - lead_in + groups - 1) // groups, 0)
     starts = jnp.cumsum(shares, axis=0) - shares
     placed = deal(attended, new_counts, lead_in, shares, starts, totals, balanced)
-    summed = head_total(project(placed, out_weight)).astype(jnp.bfloat16)
+    summed = project_and_sum(placed, out_weight)
     hidden = (residual.astype(jnp.float32) + summed.astype(jnp.float32)).astype(jnp.bfloat16)
     return (hidden, gathered_keys, gathered_values)
 
 
 def solution(mesh):
+    req_size = mesh.shape["req"]
+    split_mesh = Mesh(
+        mesh.devices.reshape(req_size // 2, 2, mesh.shape["head"]), ("chip", "core", "head")
+    )
     placed = (
-        P("req", "head"),
-        P("req", "head"),
-        P("req", "head"),
-        P("req", None, "head"),
-        P("req", None, "head"),
-        P("req", None),
-        P("req"),
-        P("req"),
-        P("req"),
-        P("req", "head"),
-        P("head", "req"),
+        P(REQ, "head"),
+        P(REQ, "head"),
+        P(REQ, "head"),
+        P(REQ, None, "head"),
+        P(REQ, None, "head"),
+        P(REQ, None),
+        P(REQ),
+        P(REQ),
+        P(REQ),
+        P(REQ, "head"),
+        P("head", REQ),
     )
     return jax.shard_map(
         local,
-        mesh=mesh,
+        mesh=split_mesh,
         in_specs=placed,
-        out_specs=(P("req", "head"), P("req", None, "head"), P("req", None, "head")),
+        out_specs=(P(REQ, "head"), P(REQ, None, "head"), P(REQ, None, "head")),
         check_vma=False,
     )

time: 301 us -> 416 us (1.38)
  waiting for transfers between devices: 175 us -> 275 us
  local copies, waits for them, and re-layouts: 35 us -> 46.3 us
  blocking collectives: 9.49 us -> 15.2 us
    all_gather x1 -> x2, waiting for transfers between devices: 46.7 us -> 170 us  [the longest x1 160 us: project_and_sum(): weight_part = lax.all_gather(out_weight, 'chip', axis=1, tiled=True)]
    all_to_all x1, waiting for transfers between devices: 48.8 us -> 25.9 us  [deal(): lax.all_to_all(outgoing, REQ, split_axis=0, concat_axis=0, tiled=True)]
    all_to_all x0 -> x1, blocking collectives: none -> 5.71 us  [project_and_sum(): lax.all_to_all(reduced, 'core', split_axis=0, concat_axis=0, tiled=True)]
  transfers between devices with their start and end apart: 3 -> 4, of which waited for: 3 -> 4; matrix products, arithmetic and copies ran while one was open for 13% -> 0% of each run, Pallas kernels for 13% -> 0%
where the time goes in v4:
time: 416 us; the launch traced here: 415 us
  waiting for transfers between devices  275 us (66%)
  local copies, waits for them, and re-layouts  46.3 us (11%)
  Pallas kernels  38.5 us (9%)
  between operations  15.3 us (4%)
  blocking collectives  15.2 us (4%)
  matrix products  13.3 us (3%)
  other arithmetic  7.06 us (2%)
    all_gather x1, waiting for transfers between devices, project_and_sum(): weight_part = lax.all_gather(out_weight, 'chip', axis=1, tiled=True)  160 us
    reduce_scatter x1, waiting for transfers between devices, project_and_sum(): lax.psum_scatter(jnp.moveaxis(partial_sum, 1, 0), 'head', scatter_dimensi...  79.1 us
    pallas_call x1, Pallas kernels, paged_attention(): pl.pallas_call(kernel, grid_spec=pltpu.PrefetchScalarGridSpec(num_scalar_...  38.5 us
    all_to_all x1, waiting for transfers between devices, deal(): lax.all_to_all(outgoing, REQ, split_axis=0, concat_axis=0, tiled=True)  25.9 us
    dot_general x1, matrix products, project_and_sum(): jnp.dot(both_rows, weight_part, preferred_element_type=jnp.float32)  13.3 us
    unnamed x1, blocking collectives  9.49 us
    all_gather x1, waiting for transfers between devices, project_and_sum(): both_rows = lax.all_gather(row_block, 'core', axis=0, tiled=True)  9.41 us
  transfers between devices with their start and end apart: 4, of which 4 were waited for; matrix products, arithmetic and copies ran while one was open for 0% of the time, Pallas kernels for 0%

profile of v4, /device:TPU:0, one launch (start us, length us, event | category | flops | bytes accessed | tf_op | source)
XLA Modules:
  0.0 415.1 jit_solution(4253285938033131036)
XLA Ops:
  7.2 2.9 copy.40
  13.3 0.8 dynamic-update-slice.1
  14.1 9.5 %all-reduce.2 = (s32[16]{0:T(128)S(1)}, s32[8]{0:T(128)S(1)}) all-reduce(s32[16]{0:T(128)S(1)} %dynamic-update-slice, s32[8]{0:T(128)S(1)} %dynamic-update-slice.1), channel_id=1, replica_groups=mesh['chip'=4,'core'=2,'head'=4] {'chip','core'}, use_global_device_ids=true, to_apply=%add | all-reduce | flops 24 | bytes 192
  24.9 4.7 %gather_fusion.4 = s32[512]{0:T(512)S(1)} fusion(s32[2,14]{1,0:T(2,128)S(1)} %copy-done, s32[512]{0:T(512)S(1)} %bitcast.71), kind=kCustom, calls=%fused_computation.4 | custom fusion | bytes 8192 | tf_op jit(solution)/shard_map/jit(take_along_axis)/gather | solution.py:141
  29.8 3.3 gather_fusion
  34.8 5.4 %scatter_fusion = bf16[3584,256]{1,0:T(8,128)(2,1)} fusion(bf16[3584,256]{1,0:T(8,128)(2,1)} %bitcast.8, s32[512]{0:T(512)S(1)} %bitcast.85, bf16[512,256]{1,0:T(8,128)(2,1)S(1)} %copy-done.4), kind=kCustom, calls=%fused_computation.5 | custom fusion | bytes 788480 | tf_op jit(solution)/shard_map/scatter | solution.py:148
  40.2 3.6 gather_fusion.1
  43.7 3.6 scatter_fusion.1
  47.3 1.9 gather_fusion.2
  49.3 38.5 %shard_map.130 = bf16[512,2048]{1,0:T(8,128)(2,1)} custom-call(s32[2]{0:T(128)} %refs_0_.1, bf16[512,2048]{1,0:T(8,128)(2,1)} %refs_1_.1, bf16[2,1792,256]{2,1,0:T(8,128)(2,1)} %bitcast.79, bf16[2,1792,256]{2,1,0:T(8,128)(2,1)} %bitcast.80), custom_call_target="tpu_custom_call" | custom-call | tf_op jit(solution)/shard_map/pallas_call | solution.py:49
  87.7 7.1 %gather_fusion.3 = bf16[512,2048]{1,0:T(8,128)(2,1)} fusion(bf16[512,2048]{1,0:T(8,128)(2,1)} %shard_map.130, s32[1024]{0:T(1024)S(1)} %pad_clamp_fusion), kind=kCustom, calls=%fused_computation.3 | custom fusion | bytes 4196352 | tf_op jit(solution)/shard_map/jit(_take)/gather | solution.py:87
  94.8 3.3 select_select_fusion
  98.1 3.6 all-to-all-start
  102.4 25.9 %all-to-all-done = bf16[8,64,2048]{2,1,0:T(8,128)(2,1)S(1)} async-done(((bf16[8,64,2048]{2,1,0:T(8,128)(2,1)}), bf16[8,64,2048]{2,1,0:T(8,128)(2,1)S(1)}, u32[]{:S(2)}, u32[]{:S(2)}) %all-to-all-start) | async-done | bytes 2097184 | tf_op jit(solution)/shard_map/all_to_all | solution.py:89
  128.3 4.5 %scatter_custom_fusion.2 = bf16[264,2048]{1,0:T(8,128)(2,1)} fusion(s32[512]{0:T(512)S(1)} %bitcast.93, bf16[512,2048]{1,0:T(8,128)(2,1)S(1)} %bitcast.82, bf16[]{:T(256)} %constant.127.clone.1), kind=kCustom, calls=%fused_computation.13 | custom fusion | bytes 1081346 | tf_op jit(solution)/shard_map/scatter | solution.py:95
  133.6 9.4 %all-gather.3.cloned.1.call-done = bf16[528,2048]{1,0:T(8,128)(2,1)} async-done(((bf16[264,2048]{1,0:T(8,128)(2,1)}), bf16[528,2048]{1,0:T(8,128)(2,1)}) %all-gather.3.cloned.1.call-update) | async-done | bytes 2162704 | tf_op jit(solution)/shard_map/all_gather | solution.py:104
  143.0 160.3 %all-gather.5.cloned.1.call-done = bf16[2048,4096]{1,0:T(8,128)(2,1)} async-done(((bf16[2048,1024]{1,0:T(8,128)(2,1)}), bf16[2048,4096]{1,0:T(8,128)(2,1)}) %all-gather.5.cloned.1.call-update) | async-done | bytes 16777232 | tf_op jit(solution)/shard_map/all_gather | solution.py:103
  303.4 13.3 %convolution_convert_fusion = bf16[528,4096]{1,0:T(8,128)(2,1)S(1)} fusion(bf16[528,2048]{1,0:T(8,128)(2,1)} %all-gather.3.cloned.1.call-done, bf16[2048,4096]{1,0:T(8,128)(2,1)} %all-gather.5.cloned.1.call-done), kind=kOutput, calls=%fused_computation.8 | convolution fusion | flops 8860532736 | bytes 23265280 | tf_op jit(solution)/shard_map/dot_general | solution.py:105
  316.7 2.6 copy.32
  319.3 79.1 %reduce-scatter.2.cloned.1.call-done = bf16[1,528,1024]{2,1,0:T(8,128)(2,1)} async-done(((bf16[4,528,1024]{2,1,0:T(8,128)(2,1)}), bf16[1,528,1024]{2,1,0:T(8,128)(2,1)}) %reduce-scatter.2.cloned.1.call-update) | async-done | bytes 1081360 | tf_op jit(solution)/shard_map/reduce_scatter | solution.py:108
  398.4 5.7 %all_to_all.10 = bf16[2,264,1,1024]{3,1,2,0:T(8,128)(2,1)S(1)} all-to-all(bf16[2,264,1,1024]{3,1,2,0:T(8,128)(2,1)} %bitcast.83), channel_id=1, replica_groups=mesh['chip'=4,'core'=2,'head'=4] {'core'}, dimensions={0} | all-to-all | bytes 2162688 | tf_op jit(solution)/shard_map/all_to_all | solution.py:111
  404.3 1.7 copy.23
  406.0 0.9 copy.30
  407.2 1.3 add_convert_fusion
  (69 shorter events, 6.9 us)
Async XLA Ops:
  10.1 0.7 copy-start.6
  10.1 1.5 copy-start.7
  10.1 1.8 copy-start.8
  10.1 14.7 %copy-start = (s32[2,14]{1,0:T(2,128)S(1)}, s32[2,14]{1,0:T(2,128)}, u32[]{:S(2)}) copy-start(s32[2,14]{1,0:T(2,128)} %param.16) | copy-start | bytes 340
  29.8 5.0 %copy-start.4 = (bf16[512,256]{1,0:T(8,128)(2,1)S(1)}, bf16[512,256]{1,0:T(8,128)(2,1)}, u32[]{:S(2)}) copy-start(bf16[512,256]{1,0:T(8,128)(2,1)} %param.12) | copy-start | bytes 786436
  40.2 3.6 copy-start.2
  40.2 3.6 copy-start.5
  47.3 40.4 %copy-start.1 = (bf16[3584,256]{1,0:T(8,128)(2,1)}, bf16[3584,256]{1,0:T(8,128)(2,1)S(1)}, u32[]{:S(2)}) copy-start(bf16[3584,256]{1,0:T(8,128)(2,1)S(1)} %scatter_fusion.1) | copy-start | bytes 5505028
  98.1 30.2 %all-to-all-start = ((bf16[8,64,2048]{2,1,0:T(8,128)(2,1)}), bf16[8,64,2048]{2,1,0:T(8,128)(2,1)S(1)}, u32[]{:S(2)}, u32[]{:S(2)}) async-start(bf16[8,64,2048]{2,1,0:T(8,128)(2,1)} %select_select_fusion), calls=%async_computation | async-start | bytes 4194304 | tf_op jit(solution)/shard_map/all_to_all | solution.py:89
  101.7 41.3 %all-gather.3.cloned.1.call-start = ((), (), s32[]{:S(2)}) async-start(), calls=%async_computation.3 | async-start | bytes 3244032 | tf_op jit(solution)/shard_map/all_gather | solution.py:104
  132.8 170.6 %all-gather.5.cloned.1.call-start = ((), (), s32[]{:S(2)}) async-start(), calls=%async_computation.4 | async-start | bytes 20971520 | tf_op jit(solution)/shard_map/all_gather | solution.py:103
  133.6 264.8 %reduce-scatter.2.cloned.1.call-start = ((), (), s32[]{:S(2)}) async-start(), calls=%async_computation.5 | async-start | bytes 5406720 | tf_op jit(solution)/shard_map/reduce_scatter | solution.py:108
  406.0 1.2 copy-start.3
Sparse Core Ops, SparseCore 0:
  132.9 10.0 all-gather.2
  144.9 158.4 all-gather.4
  319.4 78.9 reduce-scatter.1

commit v5 on v2

--- a/solution.py
+++ b/solution.py
@@ -94,18 +94,23 @@
     return blank_rows.at[landing.reshape(-1)].set(arrived.reshape(-1, columns), mode="drop")
 
 
-def project(row_block, out_weight):
-    return jnp.dot(
-        row_block,
-        lax.all_gather(out_weight, "req", axis=1, tiled=True),
-        preferred_element_type=jnp.float32,
-    )
-
-
-def head_total(partial_sum):
-    return lax.psum_scatter(
-        partial_sum.astype(jnp.bfloat16), "head", scatter_dimension=1, tiled=True
-    ).astype(jnp.float32)
+def project_and_sum(row_block, out_weight, pieces=2):
+    head_groups = lax.axis_size("head")
+    groups = lax.axis_size("req")
+    rows = row_block.shape[0]
+    block_cols = out_weight.shape[1]
+    width = block_cols // pieces
+    reduced = []
+    for piece in range(pieces):
+        weight_part = lax.all_gather(
+            out_weight[:, piece * width : (piece + 1) * width], "req", axis=1, tiled=True
+        )
+        partial_sum = jnp.dot(row_block, weight_part, preferred_element_type=jnp.float32)
+        summed = lax.psum_scatter(
+            partial_sum.astype(jnp.bfloat16), "head", scatter_dimension=1, tiled=True
+        )
+        reduced.append(summed.reshape(rows, groups // head_groups, width))
+    return jnp.stack(reduced, axis=2).reshape(rows, -1)
 
 
 def local(
@@ -164,7 +169,7 @@
     shares = jnp.maximum((totals[:, None] - lead_in + groups - 1) // groups, 0)
     starts = jnp.cumsum(shares, axis=0) - shares
     placed = deal(attended, new_counts, lead_in, shares, starts, totals, balanced)
-    summed = head_total(project(placed, out_weight)).astype(jnp.bfloat16)
+    summed = project_and_sum(placed, out_weight)
     hidden = (residual.astype(jnp.float32) + summed.astype(jnp.float32)).astype(jnp.bfloat16)
     return (hidden, gathered_keys, gathered_values)
 

time: 301 us -> 319 us (1.060)
  local copies, waits for them, and re-layouts: 35 us -> 50.3 us
  matrix products: 16.5 us -> 19.7 us
    all_to_all x1, waiting for transfers between devices: 48.8 us -> 31.3 us  [deal(): lax.all_to_all(outgoing, 'req', split_axis=0, concat_axis=0, tiled=True)]
    all_gather x1 -> x2, waiting for transfers between devices: 46.7 us -> 61 us  [project_and_sum(): lax.all_gather(out_weight[:, piece * width:(piece + 1) * width], 'req', a...]
    convert_element_type x0 -> x2, local copies, waits for them, and re-layouts: none -> 4.88 us  [local(): summed.astype(jnp.float32)]
    another operation x0 -> x4, local copies, waits for them, and re-layouts: none -> 4.32 us  [project_and_sum(): return jnp.stack(reduced, axis=2).reshape(rows, -1)]
    dot_general x1 -> x2, matrix products: 16.5 us -> 19.7 us  [project_and_sum(): jnp.dot(row_block, weight_part, preferred_element_type=jnp.float32)]
    reduce_scatter x1 -> x2, waiting for transfers between devices: 79.1 us -> 81 us  [project_and_sum(): lax.psum_scatter(partial_sum.astype(jnp.bfloat16), 'head', scatter_dimens...]
  transfers between devices with their start and end apart: 3 -> 5, of which waited for: 3 -> 4; matrix products, arithmetic and copies ran while one was open for 13% -> 19% of each run, Pallas kernels for 13% -> 12%
where the time goes in v5:
time: 319 us; the launch traced here: 318 us
  waiting for transfers between devices  174 us (55%)
  local copies, waits for them, and re-layouts  50.3 us (16%)
  Pallas kernels  38.4 us (12%)
  matrix products  19.7 us (6%)
  between operations  15.3 us (5%)
  blocking collectives  9.49 us (3%)
  other arithmetic  6.92 us (2%)
  starting transfers between devices  3.98 us (1%)
    reduce_scatter x2, waiting for transfers between devices, project_and_sum(): lax.psum_scatter(partial_sum.astype(jnp.bfloat16), 'head', scatter_dimens...  81 us
    all_gather x2, waiting for transfers between devices, project_and_sum(): lax.all_gather(out_weight[:, piece * width:(piece + 1) * width], 'req', a...  61 us
    pallas_call x1, Pallas kernels, paged_attention(): pl.pallas_call(kernel, grid_spec=pltpu.PrefetchScalarGridSpec(num_scalar_...  38.4 us
    all_to_all x1, waiting for transfers between devices, deal(): lax.all_to_all(outgoing, 'req', split_axis=0, concat_axis=0, tiled=True)  31.3 us
    dot_general x2, matrix products, project_and_sum(): jnp.dot(row_block, weight_part, preferred_element_type=jnp.float32)  19.7 us
    unnamed x1, blocking collectives  9.49 us
  transfers between devices with their start and end apart: 5, of which 4 were waited for; matrix products, arithmetic and copies ran while one was open for 19% of the time, Pallas kernels for 12%

profile of v5, /device:TPU:0, one launch (start us, length us, event | category | flops | bytes accessed | tf_op | source)
XLA Modules:
  0.0 318.3 jit_solution(1696191938071594728)
XLA Ops:
  7.2 3.1 copy.32
  10.3 2.2 fusion.18
  16.2 9.5 %all-reduce.2 = (s32[16]{0:T(128)S(1)}, s32[8]{0:T(128)S(1)}) all-reduce(s32[16]{0:T(128)S(1)} %dynamic-update-slice, s32[8]{0:T(128)S(1)} %dynamic-update-slice.1), channel_id=1, replica_groups=mesh['req'=8,'head'=4] {'req'}, use_global_device_ids=true, to_apply=%add | all-reduce | flops 24 | bytes 192
  26.2 4.8 %gather_fusion.4 = s32[512]{0:T(512)S(1)} fusion(s32[2,14]{1,0:T(2,128)S(1)} %copy-done, s32[512]{0:T(512)S(1)} %bitcast.57), kind=kCustom, calls=%fused_computation.4 | custom fusion | bytes 8192 | tf_op jit(solution)/shard_map/jit(take_along_axis)/gather | solution.py:142
  32.4 3.3 %gather_fusion = s32[512]{0:T(512)S(1)} fusion(s32[2]{0:T(128)S(1)} %bitcast_subtract_fusion, s32[1024]{0:T(1024)S(1)} %pad_clamp_fusion.2), kind=kCustom, calls=%fused_computation | custom fusion | bytes 6144 | tf_op jit(solution)/shard_map/jit(_take)/gather | solution.py:82
  35.9 5.4 %scatter_fusion = bf16[3584,256]{1,0:T(8,128)(2,1)} fusion(bf16[3584,256]{1,0:T(8,128)(2,1)} %bitcast.8, s32[512]{0:T(512)S(1)} %bitcast.66, bf16[512,256]{1,0:T(8,128)(2,1)S(1)} %copy-done.5), kind=kCustom, calls=%fused_computation.5 | custom fusion | bytes 788480 | tf_op jit(solution)/shard_map/scatter | solution.py:149
  41.3 3.5 %gather_fusion.1 = bf16[28,128,256]{2,1,0:T(8,128)(2,1)} fusion(bf16[28,128,256]{2,1,0:T(8,128)(2,1)} %bitcast.11, s32[1024]{0:T(1024)S(1)} %pad_clamp_fusion.1), kind=kCustom, calls=%fused_computation.1 | custom fusion | bytes 3670128 | tf_op jit(solution)/shard_map/gather | solution.py:157
  44.9 3.6 %scatter_fusion.1 = bf16[3584,256]{1,0:T(8,128)(2,1)S(1)} fusion(bf16[3584,256]{1,0:T(8,128)(2,1)S(1)} %bitcast.60, s32[512]{0:T(512)S(1)} %bitcast.67, bf16[512,256]{1,0:T(8,128)(2,1)S(1)} %copy-done.6), kind=kCustom, calls=%fused_computation.6 | custom fusion | bytes 788480 | tf_op jit(solution)/shard_map/scatter | solution.py:151
  48.5 1.9 gather_fusion.2
  50.4 38.4 %shard_map.130 = bf16[512,2048]{1,0:T(8,128)(2,1)} custom-call(s32[2]{0:T(128)} %refs_0_.1, bf16[512,2048]{1,0:T(8,128)(2,1)} %refs_1_.1, bf16[2,1792,256]{2,1,0:T(8,128)(2,1)} %bitcast.62, bf16[2,1792,256]{2,1,0:T(8,128)(2,1)} %bitcast.63), custom_call_target="tpu_custom_call" | custom-call | tf_op jit(solution)/shard_map/pallas_call | solution.py:48
  89.5 6.3 %gather_fusion.3 = bf16[512,2048]{1,0:T(8,128)(2,1)S(1)} fusion(bf16[512,2048]{1,0:T(8,128)(2,1)} %shard_map.130, s32[1024]{0:T(1024)S(1)} %pad_clamp_fusion), kind=kCustom, calls=%fused_computation.3 | custom fusion | bytes 4196352 | tf_op jit(solution)/shard_map/jit(_take)/gather | solution.py:86
  98.1 3.6 %all-to-all-start = ((bf16[8,64,2048]{2,1,0:T(8,128)(2,1)}), bf16[8,64,2048]{2,1,0:T(8,128)(2,1)S(1)}, u32[]{:S(2)}, u32[]{:S(2)}) async-start(bf16[8,64,2048]{2,1,0:T(8,128)(2,1)} %select_select_fusion), calls=%async_computation | async-start | bytes 4194304 | tf_op jit(solution)/shard_map/all_to_all | solution.py:88
  102.4 31.3 %all-to-all-done = bf16[8,64,2048]{2,1,0:T(8,128)(2,1)S(1)} async-done(((bf16[8,64,2048]{2,1,0:T(8,128)(2,1)}), bf16[8,64,2048]{2,1,0:T(8,128)(2,1)S(1)}, u32[]{:S(2)}, u32[]{:S(2)}) %all-to-all-start) | async-done | bytes 2097184 | tf_op jit(solution)/shard_map/all_to_all | solution.py:88
  133.7 3.8 %scatter_custom_fusion.2 = bf16[264,2048]{1,0:T(8,128)(2,1)S(1)} fusion(s32[512]{0:T(512)S(1)} %bitcast.74, bf16[512,2048]{1,0:T(8,128)(2,1)S(1)} %bitcast.64, bf16[]{:T(256)} %constant.123.clone.1), kind=kCustom, calls=%fused_computation.13 | custom fusion | bytes 1081346 | tf_op jit(solution)/shard_map/scatter | solution.py:94
  137.5 9.9 %convolution_convert_fusion.1 = bf16[264,4096]{1,0:T(8,128)(2,1)} fusion(bf16[264,2048]{1,0:T(8,128)(2,1)S(1)} %scatter_custom_fusion.2, bf16[2048,4096]{1,0:T(8,128)(2,1)} %all-gather.3.cloned.1.call-done), kind=kOutput, calls=%fused_computation.9 | convolution fusion | flops 4430266368 | bytes 20021248 | tf_op jit(solution)/shard_map/dot_general | solution.py:108
  147.5 61.0 %all-gather.5.cloned.1.call-done = bf16[2048,4096]{1,0:T(8,128)(2,1)} async-done(((bf16[2048,512]{1,0:T(8,128)(2,1)}), bf16[2048,4096]{1,0:T(8,128)(2,1)}) %all-gather.5.cloned.1.call-update) | async-done | bytes 16777232 | tf_op jit(solution)/shard_map/all_gather | solution.py:105
  208.5 9.8 %convolution_convert_fusion = bf16[264,4096]{1,0:T(8,128)(2,1)} fusion(bf16[264,2048]{1,0:T(8,128)(2,1)S(1)} %scatter_custom_fusion.2, bf16[2048,4096]{1,0:T(8,128)(2,1)} %all-gather.5.cloned.1.call-done), kind=kOutput, calls=%fused_computation.8 | convolution fusion | flops 4430266368 | bytes 20021248 | tf_op jit(solution)/shard_map/dot_general | solution.py:108
  218.4 37.1 %reduce-scatter.3.cloned.1.call-done = bf16[264,1024]{1,0:T(8,128)(2,1)} async-done(((bf16[264,4096]{1,0:T(8,128)(2,1)}), bf16[264,1024]{1,0:T(8,128)(2,1)}) %reduce-scatter.3.cloned.1.call-update) | async-done | bytes 540688 | tf_op jit(solution)/shard_map/reduce_scatter | solution.py:109
  255.5 2.1 stack_reshape.6
  257.7 43.9 %reduce-scatter.5.cloned.1.call-done = bf16[264,1024]{1,0:T(8,128)(2,1)} async-done(((bf16[264,4096]{1,0:T(8,128)(2,1)}), bf16[264,1024]{1,0:T(8,128)(2,1)}) %reduce-scatter.5.cloned.1.call-update) | async-done | bytes 540688 | tf_op jit(solution)/shard_map/reduce_scatter | solution.py:109
  301.6 2.1 stack_reshape.7
  303.9 1.7 copy.19
  305.6 3.2 %reshape.601 = f32[264,2048]{1,0:T(8,128)} reshape(f32[264,2,2,512]{3,2,1,0:T(2,128)S(1)} %copy.19) | data formatting | bytes 4325376 | tf_op jit(solution)/shard_map/convert_element_type | solution.py:173
  308.8 2.9 add_convert_fusion
  (78 shorter events, 8.5 us)
Async XLA Ops:
  7.2 130.4 %all-gather.3.cloned.1.call-start = ((), (), s32[]{:S(2)}) async-start(), calls=%async_computation.3 | async-start | bytes 18874368 | tf_op jit(solution)/shard_map/all_gather | solution.py:105
  7.2 3.1 copy-start.3
  12.5 1.4 copy-start.9
  12.5 3.5 %copy-start.8 = (s32[2]{0:T(128)S(1)}, s32[2]{0:T(128)}, u32[]{:S(2)}) copy-start(s32[2]{0:T(128)} %param.17) | copy-start | bytes 28
  12.5 13.4 %copy-start = (s32[2,14]{1,0:T(2,128)S(1)}, s32[2,14]{1,0:T(2,128)}, u32[]{:S(2)}) copy-start(s32[2,14]{1,0:T(2,128)} %param.16) | copy-start | bytes 340
  12.5 13.4 %copy-start.7 = (s32[2]{0:T(128)S(1)}, s32[2]{0:T(128)}, u32[]{:S(2)}) copy-start(s32[2]{0:T(128)} %refs_0_.1) | copy-start | bytes 28
  12.6 196.0 %all-gather.5.cloned.1.call-start = ((), (), s32[]{:S(2)}) async-start(), calls=%async_computation.5 | async-start | bytes 18874368 | tf_op jit(solution)/shard_map/all_gather | solution.py:105
  32.4 3.6 %copy-start.5 = (bf16[512,256]{1,0:T(8,128)(2,1)S(1)}, bf16[512,256]{1,0:T(8,128)(2,1)}, u32[]{:S(2)}) copy-start(bf16[512,256]{1,0:T(8,128)(2,1)} %param.12) | copy-start | bytes 786436
  41.3 3.6 %copy-start.2 = (bf16[28,128,256]{2,1,0:T(8,128)(2,1)S(1)}, bf16[28,128,256]{2,1,0:T(8,128)(2,1)}, u32[]{:S(2)}) copy-start(bf16[28,128,256]{2,1,0:T(8,128)(2,1)} %param.15) | copy-start | bytes 5505028
  41.3 3.6 %copy-start.6 = (bf16[512,256]{1,0:T(8,128)(2,1)S(1)}, bf16[512,256]{1,0:T(8,128)(2,1)}, u32[]{:S(2)}) copy-start(bf16[512,256]{1,0:T(8,128)(2,1)} %param.13) | copy-start | bytes 786436
  48.4 40.4 %copy-start.1 = (bf16[3584,256]{1,0:T(8,128)(2,1)}, bf16[3584,256]{1,0:T(8,128)(2,1)S(1)}, u32[]{:S(2)}) copy-start(bf16[3584,256]{1,0:T(8,128)(2,1)S(1)} %scatter_fusion.1) | copy-start | bytes 5505028
  98.1 35.6 %all-to-all-start = ((bf16[8,64,2048]{2,1,0:T(8,128)(2,1)}), bf16[8,64,2048]{2,1,0:T(8,128)(2,1)S(1)}, u32[]{:S(2)}, u32[]{:S(2)}) async-start(bf16[8,64,2048]{2,1,0:T(8,128)(2,1)} %select_select_fusion), calls=%async_computation | async-start | bytes 4194304 | tf_op jit(solution)/shard_map/all_to_all | solution.py:88
  101.7 153.8 %reduce-scatter.3.cloned.1.call-start = ((), (), s32[]{:S(2)}) async-start(), calls=%async_computation.4 | async-start | bytes 2703360 | tf_op jit(solution)/shard_map/reduce_scatter | solution.py:109
  147.5 154.1 %reduce-scatter.5.cloned.1.call-start = ((), (), s32[]{:S(2)}) async-start(), calls=%async_computation.6 | async-start | bytes 2703360 | tf_op jit(solution)/shard_map/reduce_scatter | solution.py:109
  305.6 3.2 %copy-start.4 = (bf16[264,2048]{1,0:T(8,128)(2,1)S(1)}, bf16[264,2048]{1,0:T(8,128)(2,1)}, u32[]{:S(2)}) copy-start(bf16[264,2048]{1,0:T(8,128)(2,1)} %param.20) | copy-start | bytes 3244036
Sparse Core Ops, SparseCore 0:
  12.7 95.7 all-gather.2
  110.4 98.1 all-gather.4
  210.8 44.6 reduce-scatter.2
  257.7 43.8 reduce-scatter.4

commit v6 on v2

--- a/solution.py
+++ b/solution.py
@@ -95,11 +95,9 @@
 
 
 def project(row_block, out_weight):
-    return jnp.dot(
-        row_block,
-        lax.all_gather(out_weight, "req", axis=1, tiled=True),
-        preferred_element_type=jnp.float32,
-    )
+    blocks = lax.all_gather(out_weight, "req", axis=0, tiled=False)
+    product = jnp.einsum("rk,ckn->rcn", row_block, blocks, preferred_element_type=jnp.float32)
+    return product.reshape(row_block.shape[0], -1)
 
 
 def head_total(partial_sum):

time: 301 us -> 302 us (level)
  transfers between devices with their start and end apart: 3 -> 3, of which waited for: 3 -> 3; matrix products, arithmetic and copies ran while one was open for 13% -> 12% of each run, Pallas kernels for 13% -> 13%
where the time goes in v6:
time: 302 us
  waiting for transfers between devices  175 us (58%)
  Pallas kernels  38.5 us (13%)
  local copies, waits for them, and re-layouts  37.4 us (12%)
  between operations  15.8 us (5%)
  matrix products  15.2 us (5%)
  blocking collectives  9.49 us (3%)
  other arithmetic  6.52 us (2%)
  starting transfers between devices  3.9 us (1%)
    reduce_scatter x1, waiting for transfers between devices, head_total(): lax.psum_scatter(partial_sum.astype(jnp.bfloat16), 'head', scatter_dimens...  79.1 us
    all_to_all x1, waiting for transfers between devices, deal(): lax.all_to_all(outgoing, 'req', split_axis=0, concat_axis=0, tiled=True)  48.7 us
    all_gather x1, waiting for transfers between devices, project(): blocks = lax.all_gather(out_weight, 'req', axis=0, tiled=False)  46.7 us
    pallas_call x1, Pallas kernels, paged_attention(): pl.pallas_call(kernel, grid_spec=pltpu.PrefetchScalarGridSpec(num_scalar_...  38.5 us
    dot_general x1, matrix products, project(): jnp.einsum('rk,ckn->rcn', row_block, blocks, preferred_element_type=jnp.f...  15.2 us
    unnamed x1, blocking collectives  9.49 us
    gather x1, local copies, waits for them, and re-layouts, deal(): jnp.take(row_block, source.reshape(-1), axis=0)  6.27 us
  transfers between devices with their start and end apart: 3, of which 3 were waited for; matrix products, arithmetic and copies ran while one was open for 12% of the time, Pallas kernels for 13%

profile of v6, /device:TPU:0, one launch (start us, length us, event | category | flops | bytes accessed | tf_op | source)
XLA Modules:
  0.0 301.9 jit_solution(16920928787083422673)
XLA Ops:
  7.3 0.6 all-gather.3.cloned.1.call-update
  8.7 0.6 dynamic-slice
  10.2 0.8 dynamic-update-slice.1
  11.0 9.5 %all-reduce.2 = (s32[16]{0:T(128)S(1)}, s32[8]{0:T(128)S(1)}) all-reduce(s32[16]{0:T(128)S(1)} %dynamic-update-slice, s32[8]{0:T(128)S(1)} %dynamic-update-slice.1), channel_id=1, replica_groups=mesh['req'=8,'head'=4] {'req'}, use_global_device_ids=true, to_apply=%add | all-reduce | flops 24 | bytes 192
  22.3 4.8 %gather_fusion.4 = s32[512]{0:T(512)S(1)} fusion(s32[2,14]{1,0:T(2,128)S(1)} %copy-done, s32[512]{0:T(512)S(1)} %bitcast.58), kind=kCustom, calls=%fused_computation.4 | custom fusion | bytes 8192 | tf_op jit(solution)/shard_map/jit(take_along_axis)/gather | solution.py:135
  27.3 3.4 %scatter_fusion = bf16[3584,256]{1,0:T(8,128)(2,1)S(1)} fusion(bf16[3584,256]{1,0:T(8,128)(2,1)S(1)} %bitcast.64, s32[512]{0:T(512)S(1)} %bitcast.71, bf16[512,256]{1,0:T(8,128)(2,1)S(1)} %copy-done.6), kind=kCustom, calls=%fused_computation.5 | custom fusion | bytes 788480 | tf_op jit(solution)/shard_map/scatter | solution.py:142
  30.7 1.2 copy-done.3
  31.9 3.6 %gather_fusion.1 = bf16[28,128,256]{2,1,0:T(8,128)(2,1)} fusion(bf16[28,128,256]{2,1,0:T(8,128)(2,1)} %bitcast.62, s32[1024]{0:T(1024)S(1)} %pad_clamp_fusion.1), kind=kCustom, calls=%fused_computation.1 | custom fusion | bytes 3670128 | tf_op jit(solution)/shard_map/gather | solution.py:150
  35.5 3.6 %scatter_fusion.1 = bf16[3584,256]{1,0:T(8,128)(2,1)S(1)} fusion(bf16[3584,256]{1,0:T(8,128)(2,1)S(1)} %bitcast.61, s32[512]{0:T(512)S(1)} %bitcast.72, bf16[512,256]{1,0:T(8,128)(2,1)S(1)} %copy-done.7), kind=kCustom, calls=%fused_computation.6 | custom fusion | bytes 788480 | tf_op jit(solution)/shard_map/scatter | solution.py:144
  39.1 1.9 gather_fusion.2
  41.0 3.3 %gather_fusion = s32[512]{0:T(512)S(1)} fusion(s32[2]{0:T(128)S(1)} %bitcast_subtract_fusion, s32[1024]{0:T(1024)S(1)} %pad_clamp_fusion.2), kind=kCustom, calls=%fused_computation | custom fusion | bytes 6144 | tf_op jit(solution)/shard_map/jit(_take)/gather | solution.py:82
  44.4 38.5 %shard_map.130 = bf16[512,2048]{1,0:T(8,128)(2,1)} custom-call(s32[2]{0:T(128)} %refs_0_.1, bf16[512,2048]{1,0:T(8,128)(2,1)} %refs_1_.1, bf16[2,1792,256]{2,1,0:T(8,128)(2,1)} %bitcast.67, bf16[2,1792,256]{2,1,0:T(8,128)(2,1)} %bitcast.68), custom_call_target="tpu_custom_call" | custom-call | tf_op jit(solution)/shard_map/pallas_call | solution.py:48
  82.9 0.7 compare_select_fusion
  83.6 6.3 %gather_fusion.3 = bf16[512,2048]{1,0:T(8,128)(2,1)S(1)} fusion(bf16[512,2048]{1,0:T(8,128)(2,1)} %shard_map.130, s32[1024]{0:T(1024)S(1)} %pad_clamp_fusion), kind=kCustom, calls=%fused_computation.3 | custom fusion | bytes 4196352 | tf_op jit(solution)/shard_map/jit(_take)/gather | solution.py:86
  89.9 0.7 add_compare_fusion
  90.6 1.6 select_select_fusion
  92.2 3.6 %all-to-all-start = ((bf16[8,64,2048]{2,1,0:T(8,128)(2,1)}), bf16[8,64,2048]{2,1,0:T(8,128)(2,1)S(1)}, u32[]{:S(2)}, u32[]{:S(2)}) async-start(bf16[8,64,2048]{2,1,0:T(8,128)(2,1)} %select_select_fusion), calls=%async_computation | async-start | bytes 4194304 | tf_op jit(solution)/shard_map/all_to_all | solution.py:88
  96.5 48.7 %all-to-all-done = bf16[8,64,2048]{2,1,0:T(8,128)(2,1)S(1)} async-done(((bf16[8,64,2048]{2,1,0:T(8,128)(2,1)}), bf16[8,64,2048]{2,1,0:T(8,128)(2,1)S(1)}, u32[]{:S(2)}, u32[]{:S(2)}) %all-to-all-start) | async-done | bytes 2097184 | tf_op jit(solution)/shard_map/all_to_all | solution.py:88
  145.2 3.8 %scatter_custom_fusion.2 = bf16[264,2048]{1,0:T(8,128)(2,1)S(1)} fusion(s32[512]{0:T(512)S(1)} %bitcast.79, bf16[512,2048]{1,0:T(8,128)(2,1)S(1)} %bitcast.69, bf16[]{:T(256)} %constant.123.clone.1), kind=kCustom, calls=%fused_computation.12 | custom fusion | bytes 1081346 | tf_op jit(solution)/shard_map/scatter | solution.py:94
  149.0 46.7 %all-gather.3.cloned.1.call-done = bf16[16384,1024]{1,0:T(8,128)(2,1)} async-done(((bf16[2048,1024]{1,0:T(8,128)(2,1)}), bf16[16384,1024]{1,0:T(8,128)(2,1)}) %all-gather.3.cloned.1.call-update) | async-done | bytes 33554448 | tf_op jit(solution)/shard_map/all_gather | solution.py:98
  195.8 15.2 %convert_bitcast_fusion = bf16[8,33,8,1024]{3,2,1,0:T(8,128)(2,1)S(1)} fusion(bf16[8,2048,1024]{2,1,0:T(8,128)(2,1)} %bitcast.82, bf16[264,2048]{1,0:T(8,128)(2,1)S(1)} %scatter_custom_fusion.2), kind=kOutput, calls=%fused_computation.8 | convolution fusion | flops 8860532736 | bytes 38961152 | tf_op jit(solution)/shard_map/rk,ckn->rcn/dot_general | solution.py:99
  210.9 2.4 copy.16
  213.4 79.1 %reduce-scatter.2.cloned.1.call-done = bf16[264,2048]{1,0:T(8,128)(2,1)} async-done(((bf16[264,8192]{1,0:T(8,128)(2,1)}), bf16[264,2048]{1,0:T(8,128)(2,1)}) %reduce-scatter.2.cloned.1.call-update) | async-done | bytes 1081360 | tf_op jit(solution)/shard_map/reduce_scatter | solution.py:104
  292.5 2.6 add_convert_fusion
  (65 shorter events, 3.0 us)
Async XLA Ops:
  7.2 188.6 %all-gather.3.cloned.1.call-start = ((), (), s32[]{:S(2)}) async-start(), calls=%async_computation.3 | async-start | bytes 37748736 | tf_op jit(solution)/shard_map/all_gather | solution.py:98
  7.2 1.5 copy-start.10
  7.2 2.8 copy-start.9
  7.2 14.8 %copy-start.8 = (s32[2]{0:T(128)S(1)}, s32[2]{0:T(128)}, u32[]{:S(2)}) copy-start(s32[2]{0:T(128)} %refs_0_.1) | copy-start | bytes 28
  7.2 15.1 %copy-start = (s32[2,14]{1,0:T(2,128)S(1)}, s32[2,14]{1,0:T(2,128)}, u32[]{:S(2)}) copy-start(s32[2,14]{1,0:T(2,128)} %param.16) | copy-start | bytes 340
  7.9 19.3 %copy-start.4 = (bf16[28,128,256]{2,1,0:T(8,128)(2,1)S(1)}, bf16[28,128,256]{2,1,0:T(8,128)(2,1)}, u32[]{:S(2)}) copy-start(bf16[28,128,256]{2,1,0:T(8,128)(2,1)} %param.14) | copy-start | bytes 5505028
  7.9 19.3 %copy-start.6 = (bf16[512,256]{1,0:T(8,128)(2,1)S(1)}, bf16[512,256]{1,0:T(8,128)(2,1)}, u32[]{:S(2)}) copy-start(bf16[512,256]{1,0:T(8,128)(2,1)} %param.12) | copy-start | bytes 786436
  30.6 1.2 copy-start.3
  31.9 3.6 %copy-start.2 = (bf16[28,128,256]{2,1,0:T(8,128)(2,1)S(1)}, bf16[28,128,256]{2,1,0:T(8,128)(2,1)}, u32[]{:S(2)}) copy-start(bf16[28,128,256]{2,1,0:T(8,128)(2,1)} %param.15) | copy-start | bytes 5505028
  31.9 3.6 %copy-start.7 = (bf16[512,256]{1,0:T(8,128)(2,1)S(1)}, bf16[512,256]{1,0:T(8,128)(2,1)}, u32[]{:S(2)}) copy-start(bf16[512,256]{1,0:T(8,128)(2,1)} %param.13) | copy-start | bytes 786436
  39.0 1.9 copy-start.1
  92.2 53.0 %all-to-all-start = ((bf16[8,64,2048]{2,1,0:T(8,128)(2,1)}), bf16[8,64,2048]{2,1,0:T(8,128)(2,1)S(1)}, u32[]{:S(2)}, u32[]{:S(2)}) async-start(bf16[8,64,2048]{2,1,0:T(8,128)(2,1)} %select_select_fusion), calls=%async_computation | async-start | bytes 4194304 | tf_op jit(solution)/shard_map/all_to_all | solution.py:88
  95.8 196.6 %reduce-scatter.2.cloned.1.call-start = ((), (), s32[]{:S(2)}) async-start(), calls=%async_computation.2 | async-start | bytes 5406720 | tf_op jit(solution)/shard_map/reduce_scatter | solution.py:104
  213.4 79.1 %copy-start.5 = (bf16[264,2048]{1,0:T(8,128)(2,1)S(1)}, bf16[264,2048]{1,0:T(8,128)(2,1)}, u32[]{:S(2)}) copy-start(bf16[264,2048]{1,0:T(8,128)(2,1)} %param.20) | copy-start | bytes 3244036
Sparse Core Ops, SparseCore 0:
  9.9 185.8 all-gather.2
  213.5 78.9 reduce-scatter.1

commit v7 on v4

--- a/solution.py
+++ b/solution.py
@@ -11,7 +11,7 @@
 
 
 NEGATIVE = -1e30
-REQ = ("chip", "core")
+REQ = ("y", "x", "core")
 
 
 def attention_kernel(cached_ref, q_ref, k_ref, v_ref, o_ref, *, fanout, scale_factor):
@@ -97,10 +97,11 @@
 
 def project_and_sum(row_block, out_weight):
     head_groups = lax.axis_size("head")
-    chips = lax.axis_size("chip")
+    chips = lax.axis_size("y") * lax.axis_size("x")
     rows = row_block.shape[0]
-    inner, block_cols = out_weight.shape
-    weight_part = lax.all_gather(out_weight, "chip", axis=1, tiled=True)
+    inner = out_weight.shape[0]
+    block_cols = out_weight.shape[1] // chips
+    weight_part = out_weight
     both_rows = lax.all_gather(row_block, "core", axis=0, tiled=True)
     partial_sum = jnp.dot(both_rows, weight_part, preferred_element_type=jnp.float32)
     per_chunk = chips // head_groups
@@ -167,16 +168,21 @@
     lead_in = jnp.remainder(rank_ids[None, :] - offsets_all[:, None], groups)
     shares = jnp.maximum((totals[:, None] - lead_in + groups - 1) // groups, 0)
     starts = jnp.cumsum(shares, axis=0) - shares
+    weight_near = lax.all_gather(out_weight, "x", axis=1, tiled=True)
+    weight_near = lax.all_gather(weight_near, "y", axis=1, tiled=True)
+    weight_near, attended = lax.optimization_barrier((weight_near, attended))
     placed = deal(attended, new_counts, lead_in, shares, starts, totals, balanced)
-    summed = project_and_sum(placed, out_weight)
+    summed = project_and_sum(placed, weight_near)
     hidden = (residual.astype(jnp.float32) + summed.astype(jnp.float32)).astype(jnp.bfloat16)
     return (hidden, gathered_keys, gathered_values)
 
 
 def solution(mesh):
     req_size = mesh.shape["req"]
+    side = math.isqrt(req_size // 2)
     split_mesh = Mesh(
-        mesh.devices.reshape(req_size // 2, 2, mesh.shape["head"]), ("chip", "core", "head")
+        mesh.devices.reshape(req_size // 2 // side, side, 2, mesh.shape["head"]),
+        ("y", "x", "core", "head"),
     )
     placed = (
         P(REQ, "head"),

time: 416 us -> 483 us (1.16)
  waiting for transfers between devices: 275 us -> 348 us
    all_gather x1 -> x2, waiting for transfers between devices: 160 us -> 232 us  [the longest x1 125 us: local(): weight_near = lax.all_gather(weight_near, 'y', axis=1, tiled=True)]
  transfers between devices with their start and end apart: 4 -> 5, of which waited for: 4 -> 5; matrix products, arithmetic and copies ran while one was open for 0% -> 6% of each run, Pallas kernels for 0% -> 8%
where the time goes in v7:
time: 483 us
  waiting for transfers between devices  348 us (72%)
  local copies, waits for them, and re-layouts  45.3 us (9%)
  Pallas kernels  38.4 us (8%)
  between operations  15.3 us (3%)
  matrix products  13.3 us (3%)
  blocking collectives  13 us (3%)
  other arithmetic  5.46 us (1%)
    all_gather x1, waiting for transfers between devices, local(): weight_near = lax.all_gather(weight_near, 'y', axis=1, tiled=True)  125 us
    all_gather x1, waiting for transfers between devices, local(): weight_near = lax.all_gather(out_weight, 'x', axis=1, tiled=True)  107 us
    reduce_scatter x1, waiting for transfers between devices, project_and_sum(): lax.psum_scatter(jnp.moveaxis(partial_sum, 1, 0), 'head', scatter_dimensi...  80.2 us
    pallas_call x1, Pallas kernels, paged_attention(): pl.pallas_call(kernel, grid_spec=pltpu.PrefetchScalarGridSpec(num_scalar_...  38.4 us
    all_to_all x1, waiting for transfers between devices, deal(): lax.all_to_all(outgoing, REQ, split_axis=0, concat_axis=0, tiled=True)  25.9 us
    dot_general x1, matrix products, project_and_sum(): jnp.dot(both_rows, weight_part, preferred_element_type=jnp.float32)  13.3 us
    all_gather x1, waiting for transfers between devices, project_and_sum(): both_rows = lax.all_gather(row_block, 'core', axis=0, tiled=True)  9.89 us
  transfers between devices with their start and end apart: 5, of which 5 were waited for; matrix products, arithmetic and copies ran while one was open for 6% of the time, Pallas kernels for 8%

profile of v7, /device:TPU:0, one launch (start us, length us, event | category | flops | bytes accessed | tf_op | source)
XLA Modules:
  0.0 482.9 jit_solution(16394282856059326502)
XLA Ops:
  7.2 2.9 copy.40
  10.2 106.8 %all-gather.4.cloned.1.call-done = bf16[2048,2048]{1,0:T(8,128)(2,1)} async-done(((bf16[2048,1024]{1,0:T(8,128)(2,1)}), bf16[2048,2048]{1,0:T(8,128)(2,1)}) %all-gather.4.cloned.1.call-update) | async-done | bytes 8388624 | tf_op jit(solution)/shard_map/all_gather | solution.py:171
  120.0 7.3 %all-reduce.2 = (s32[16]{0:T(128)S(1)}, s32[8]{0:T(128)S(1)}) all-reduce(s32[16]{0:T(128)S(1)} %dynamic-update-slice, s32[8]{0:T(128)S(1)} %dynamic-update-slice.1), channel_id=1, replica_groups=mesh['y'=2,'x'=2,'core'=2,'head'=4] {'y','x','core'}, use_global_device_ids=true, to_apply=%add | all-reduce | flops 24 | bytes 192
  127.8 4.8 gather_fusion.4
  134.0 3.3 gather_fusion
  137.5 5.6 %scatter_fusion = bf16[3584,256]{1,0:T(8,128)(2,1)} fusion(bf16[3584,256]{1,0:T(8,128)(2,1)} %bitcast.8, s32[512]{0:T(512)S(1)} %bitcast.85, bf16[512,256]{1,0:T(8,128)(2,1)S(1)} %copy-done.4), kind=kCustom, calls=%fused_computation.5 | custom fusion | bytes 788480 | tf_op jit(solution)/shard_map/scatter | solution.py:149
  143.1 3.7 gather_fusion.1
  146.9 3.6 scatter_fusion.1
  150.4 2.0 gather_fusion.2
  152.4 38.4 %shard_map.130 = bf16[512,2048]{1,0:T(8,128)(2,1)} custom-call(s32[2]{0:T(128)} %refs_0_.1, bf16[512,2048]{1,0:T(8,128)(2,1)} %refs_1_.1, bf16[2,1792,256]{2,1,0:T(8,128)(2,1)} %bitcast.79, bf16[2,1792,256]{2,1,0:T(8,128)(2,1)} %bitcast.80), custom_call_target="tpu_custom_call" | custom-call | tf_op jit(solution)/shard_map/pallas_call | solution.py:49
  192.2 125.2 %all-gather.6.cloned.1.call-done = bf16[2048,4096]{1,0:T(8,128)(2,1)} async-done(((bf16[2048,2048]{1,0:T(8,128)(2,1)}), bf16[2048,4096]{1,0:T(8,128)(2,1)}) %all-gather.6.cloned.1.call-update) | async-done | bytes 16777232 | tf_op jit(solution)/shard_map/all_gather | solution.py:172
  317.5 6.3 %gather_fusion.3 = bf16[512,2048]{1,0:T(8,128)(2,1)S(1)} fusion(bf16[512,2048]{1,0:T(8,128)(2,1)} %shard_map.130, s32[1024]{0:T(1024)S(1)} %pad_clamp_fusion), kind=kCustom, calls=%fused_computation.3 | custom fusion | bytes 4196352 | tf_op jit(solution)/shard_map/jit(_take)/gather | solution.py:87
  323.7 1.7 select_select_fusion
  325.4 3.6 all-to-all-start
  329.7 25.9 %all-to-all-done = bf16[8,64,2048]{2,1,0:T(8,128)(2,1)S(1)} async-done(((bf16[8,64,2048]{2,1,0:T(8,128)(2,1)}), bf16[8,64,2048]{2,1,0:T(8,128)(2,1)S(1)}, u32[]{:S(2)}, u32[]{:S(2)}) %all-to-all-start) | async-done | bytes 2097184 | tf_op jit(solution)/shard_map/all_to_all | solution.py:89
  355.6 4.5 scatter_custom_fusion.2
  360.2 9.9 %all-gather.8.cloned.1.call-done = bf16[528,2048]{1,0:T(8,128)(2,1)} async-done(((bf16[264,2048]{1,0:T(8,128)(2,1)}), bf16[528,2048]{1,0:T(8,128)(2,1)}) %all-gather.8.cloned.1.call-update) | async-done | bytes 2162704 | tf_op jit(solution)/shard_map/all_gather | solution.py:105
  370.1 13.3 %convolution_convert_fusion = bf16[528,4096]{1,0:T(8,128)(2,1)S(1)} fusion(bf16[528,2048]{1,0:T(8,128)(2,1)} %all-gather.8.cloned.1.call-done, bf16[2048,4096]{1,0:T(8,128)(2,1)} %all-gather.6.cloned.1.call-done), kind=kOutput, calls=%fused_computation.8 | convolution fusion | flops 8860532736 | bytes 23265280 | tf_op jit(solution)/shard_map/dot_general | solution.py:106
  383.4 2.6 copy.32
  386.0 80.2 %reduce-scatter.2.cloned.1.call-done = bf16[1,528,1024]{2,1,0:T(8,128)(2,1)} async-done(((bf16[4,528,1024]{2,1,0:T(8,128)(2,1)}), bf16[1,528,1024]{2,1,0:T(8,128)(2,1)}) %reduce-scatter.2.cloned.1.call-update) | async-done | bytes 1081360 | tf_op jit(solution)/shard_map/reduce_scatter | solution.py:109
  466.2 5.7 %all_to_all.10 = bf16[2,264,1,1024]{3,1,2,0:T(8,128)(2,1)S(1)} all-to-all(bf16[2,264,1,1024]{3,1,2,0:T(8,128)(2,1)} %bitcast.83), channel_id=1, replica_groups=mesh['y'=2,'x'=2,'core'=2,'head'=4] {'core'}, dimensions={0} | all-to-all | bytes 2162688 | tf_op jit(solution)/shard_map/all_to_all | solution.py:112
  472.2 1.7 copy.23
  473.9 0.9 copy.30
  475.1 1.3 add_convert_fusion
  (72 shorter events, 6.4 us)
Async XLA Ops:
  7.2 109.9 %all-gather.4.cloned.1.call-start = ((), (), s32[]{:S(2)}) async-start(), calls=%async_computation.3 | async-start | bytes 12582912 | tf_op jit(solution)/shard_map/all_gather | solution.py:171
  10.2 307.3 %all-gather.6.cloned.1.call-start = ((), (), s32[]{:S(2)}) async-start(), calls=%async_computation.4 | async-start | bytes 25165824 | tf_op jit(solution)/shard_map/all_gather | solution.py:172
  117.0 0.7 copy-start.8
  117.0 2.7 copy-start.7
  117.0 10.5 %copy-start = (s32[2,14]{1,0:T(2,128)S(1)}, s32[2,14]{1,0:T(2,128)}, u32[]{:S(2)}) copy-start(s32[2,14]{1,0:T(2,128)} %param.16) | copy-start | bytes 340
  117.0 10.6 %copy-start.6 = (s32[2]{0:T(128)S(1)}, s32[2]{0:T(128)}, u32[]{:S(2)}) copy-start(s32[2]{0:T(128)} %refs_0_.1) | copy-start | bytes 28
  134.0 3.6 copy-start.4
  143.1 3.8 copy-start.2
  143.1 3.8 copy-start.5
  150.4 40.4 %copy-start.1 = (bf16[3584,256]{1,0:T(8,128)(2,1)}, bf16[3584,256]{1,0:T(8,128)(2,1)S(1)}, u32[]{:S(2)}) copy-start(bf16[3584,256]{1,0:T(8,128)(2,1)S(1)} %scatter_fusion.1) | copy-start | bytes 5505028
  325.4 30.2 %all-to-all-start = ((bf16[8,64,2048]{2,1,0:T(8,128)(2,1)}), bf16[8,64,2048]{2,1,0:T(8,128)(2,1)S(1)}, u32[]{:S(2)}, u32[]{:S(2)}) async-start(bf16[8,64,2048]{2,1,0:T(8,128)(2,1)} %select_select_fusion), calls=%async_computation | async-start | bytes 4194304 | tf_op jit(solution)/shard_map/all_to_all | solution.py:89
  329.0 41.0 %all-gather.8.cloned.1.call-start = ((), (), s32[]{:S(2)}) async-start(), calls=%async_computation.5 | async-start | bytes 3244032 | tf_op jit(solution)/shard_map/all_gather | solution.py:105
  360.1 106.1 %reduce-scatter.2.cloned.1.call-start = ((), (), s32[]{:S(2)}) async-start(), calls=%async_computation.6 | async-start | bytes 5406720 | tf_op jit(solution)/shard_map/reduce_scatter | solution.py:109
  473.9 1.2 copy-start.3
Sparse Core Ops, SparseCore 0:
  10.3 106.6 all-gather.3
  118.6 198.8 all-gather.5
  360.2 9.7 all-gather.7
  386.1 80.0 reduce-scatter.1

commit v8 on v2

--- a/solution.py
+++ b/solution.py
@@ -103,9 +103,13 @@
 
 
 def head_total(partial_sum):
-    return lax.psum_scatter(
-        partial_sum.astype(jnp.bfloat16), "head", scatter_dimension=1, tiled=True
-    ).astype(jnp.float32)
+    head_groups = lax.axis_size("head")
+    rows, columns = partial_sum.shape
+    terms = partial_sum.astype(jnp.bfloat16).reshape(rows, head_groups, columns // head_groups)
+    arrived = lax.all_to_all(
+        jnp.moveaxis(terms, 1, 0), "head", split_axis=0, concat_axis=0, tiled=True
+    )
+    return jnp.sum(arrived.astype(jnp.float32), axis=0)
 
 
 def local(

time: 301 us -> 324 us (1.076)
  blocking collectives: 9.49 us -> 110 us
  waiting for transfers between devices: 175 us -> 96.2 us
    all_to_all x0 -> x1, blocking collectives: none -> 101 us  [head_total(): lax.all_to_all(jnp.moveaxis(terms, 1, 0), 'head', split_axis=0, concat_ax...]
    reduce_scatter x1 -> x0, waiting for transfers between devices: 79.1 us -> none  [head_total(): lax.psum_scatter(partial_sum.astype(jnp.bfloat16), 'head', scatter_dimens...]
  transfers between devices with their start and end apart: 3 -> 2, of which waited for: 3 -> 2; matrix products, arithmetic and copies ran while one was open for 13% -> 12% of each run, Pallas kernels for 13% -> 12%
where the time goes in v8:
time: 324 us
  blocking collectives  110 us (34%)
  waiting for transfers between devices  96.2 us (30%)
  Pallas kernels  38.5 us (12%)
  local copies, waits for them, and re-layouts  35.5 us (11%)
  between operations  15.8 us (5%)
  matrix products  15.2 us (5%)
  other arithmetic  8.52 us (3%)
  starting transfers between devices  3.86 us (1%)
    all_to_all x1, blocking collectives, head_total(): lax.all_to_all(jnp.moveaxis(terms, 1, 0), 'head', split_axis=0, concat_ax...  101 us
    all_to_all x1, waiting for transfers between devices, deal(): lax.all_to_all(outgoing, 'req', split_axis=0, concat_axis=0, tiled=True)  48.8 us
    all_gather x1, waiting for transfers between devices, project(): lax.all_gather(out_weight, 'req', axis=1, tiled=True)  46.7 us
    pallas_call x1, Pallas kernels, paged_attention(): pl.pallas_call(kernel, grid_spec=pltpu.PrefetchScalarGridSpec(num_scalar_...  38.5 us
    dot_general x1, matrix products, project(): jnp.dot(row_block, lax.all_gather(out_weight, 'req', axis=1, tiled=True),...  15.2 us
    unnamed x1, blocking collectives  9.49 us
  transfers between devices with their start and end apart: 2, of which 2 were waited for; matrix products, arithmetic and copies ran while one was open for 12% of the time, Pallas kernels for 12%

profile of v8, /device:TPU:0, one launch (start us, length us, event | category | flops | bytes accessed | tf_op | source)
XLA Modules:
  0.0 323.8 jit_solution(17622235230861710080)
XLA Ops:
  7.3 0.6 all-gather.2.cloned.1.call-update
  8.7 0.6 dynamic-slice
  10.2 0.8 dynamic-update-slice.1
  11.0 9.5 %all-reduce.2 = (s32[16]{0:T(128)S(1)}, s32[8]{0:T(128)S(1)}) all-reduce(s32[16]{0:T(128)S(1)} %dynamic-update-slice, s32[8]{0:T(128)S(1)} %dynamic-update-slice.1), channel_id=1, replica_groups=mesh['req'=8,'head'=4] {'req'}, use_global_device_ids=true, to_apply=%add | all-reduce | flops 24 | bytes 192
  22.3 4.8 %gather_fusion.4 = s32[512]{0:T(512)S(1)} fusion(s32[2,14]{1,0:T(2,128)S(1)} %copy-done, s32[512]{0:T(512)S(1)} %bitcast.59), kind=kCustom, calls=%fused_computation.4 | custom fusion | bytes 8192 | tf_op jit(solution)/shard_map/jit(take_along_axis)/gather | solution.py:141
  27.3 3.4 %scatter_fusion = bf16[3584,256]{1,0:T(8,128)(2,1)S(1)} fusion(bf16[3584,256]{1,0:T(8,128)(2,1)S(1)} %bitcast.65, s32[512]{0:T(512)S(1)} %bitcast.73, bf16[512,256]{1,0:T(8,128)(2,1)S(1)} %copy-done.6), kind=kCustom, calls=%fused_computation.5 | custom fusion | bytes 788480 | tf_op jit(solution)/shard_map/scatter | solution.py:148
  30.7 1.2 copy-done.3
  31.9 3.6 %gather_fusion.1 = bf16[28,128,256]{2,1,0:T(8,128)(2,1)} fusion(bf16[28,128,256]{2,1,0:T(8,128)(2,1)} %bitcast.63, s32[1024]{0:T(1024)S(1)} %pad_clamp_fusion.1), kind=kCustom, calls=%fused_computation.1 | custom fusion | bytes 3670128 | tf_op jit(solution)/shard_map/gather | solution.py:156
  35.5 3.6 %scatter_fusion.1 = bf16[3584,256]{1,0:T(8,128)(2,1)S(1)} fusion(bf16[3584,256]{1,0:T(8,128)(2,1)S(1)} %bitcast.62, s32[512]{0:T(512)S(1)} %bitcast.74, bf16[512,256]{1,0:T(8,128)(2,1)S(1)} %copy-done.7), kind=kCustom, calls=%fused_computation.6 | custom fusion | bytes 788480 | tf_op jit(solution)/shard_map/scatter | solution.py:150
  39.1 1.9 gather_fusion.2
  41.0 3.3 %gather_fusion = s32[512]{0:T(512)S(1)} fusion(s32[2]{0:T(128)S(1)} %bitcast_subtract_fusion, s32[1024]{0:T(1024)S(1)} %pad_clamp_fusion.2), kind=kCustom, calls=%fused_computation | custom fusion | bytes 6144 | tf_op jit(solution)/shard_map/jit(_take)/gather | solution.py:82
  44.4 38.5 %shard_map.130 = bf16[512,2048]{1,0:T(8,128)(2,1)} custom-call(s32[2]{0:T(128)} %refs_0_.1, bf16[512,2048]{1,0:T(8,128)(2,1)} %refs_1_.1, bf16[2,1792,256]{2,1,0:T(8,128)(2,1)} %bitcast.68, bf16[2,1792,256]{2,1,0:T(8,128)(2,1)} %bitcast.69), custom_call_target="tpu_custom_call" | custom-call | tf_op jit(solution)/shard_map/pallas_call | solution.py:48
  82.9 0.7 compare_select_fusion
  83.6 6.3 %gather_fusion.3 = bf16[512,2048]{1,0:T(8,128)(2,1)S(1)} fusion(bf16[512,2048]{1,0:T(8,128)(2,1)} %shard_map.130, s32[1024]{0:T(1024)S(1)} %pad_clamp_fusion), kind=kCustom, calls=%fused_computation.3 | custom fusion | bytes 4196352 | tf_op jit(solution)/shard_map/jit(_take)/gather | solution.py:86
  89.9 0.7 add_compare_fusion
  90.6 1.6 select_select_fusion
  92.2 3.8 %all-to-all-start = ((bf16[8,64,2048]{2,1,0:T(8,128)(2,1)}), bf16[8,64,2048]{2,1,0:T(8,128)(2,1)S(1)}, u32[]{:S(2)}, u32[]{:S(2)}) async-start(bf16[8,64,2048]{2,1,0:T(8,128)(2,1)} %select_select_fusion), calls=%async_computation | async-start | bytes 4194304 | tf_op jit(solution)/shard_map/all_to_all | solution.py:88
  96.4 48.8 %all-to-all-done = bf16[8,64,2048]{2,1,0:T(8,128)(2,1)S(1)} async-done(((bf16[8,64,2048]{2,1,0:T(8,128)(2,1)}), bf16[8,64,2048]{2,1,0:T(8,128)(2,1)S(1)}, u32[]{:S(2)}, u32[]{:S(2)}) %all-to-all-start) | async-done | bytes 2097184 | tf_op jit(solution)/shard_map/all_to_all | solution.py:88
  145.2 3.8 %scatter_custom_fusion.2 = bf16[264,2048]{1,0:T(8,128)(2,1)S(1)} fusion(s32[512]{0:T(512)S(1)} %bitcast.81, bf16[512,2048]{1,0:T(8,128)(2,1)S(1)} %bitcast.71, bf16[]{:T(256)} %constant.125.clone.1), kind=kCustom, calls=%fused_computation.12 | custom fusion | bytes 1081346 | tf_op jit(solution)/shard_map/scatter | solution.py:94
  149.0 46.7 %all-gather.2.cloned.1.call-done = bf16[2048,8192]{1,0:T(8,128)(2,1)} async-done(((bf16[2048,1024]{1,0:T(8,128)(2,1)}), bf16[2048,8192]{1,0:T(8,128)(2,1)}) %all-gather.2.cloned.1.call-update) | async-done | bytes 33554448 | tf_op jit(solution)/shard_map/all_gather | solution.py:100
  195.8 15.2 %convolution_convert_fusion = bf16[264,8192]{1,0:T(8,128)(2,1)S(1)} fusion(bf16[264,2048]{1,0:T(8,128)(2,1)S(1)} %scatter_custom_fusion.2, bf16[2048,8192]{1,0:T(8,128)(2,1)} %all-gather.2.cloned.1.call-done), kind=kOutput, calls=%fused_computation.8 | convolution fusion | flops 8860532736 | bytes 38961152 | tf_op jit(solution)/shard_map/dot_general | solution.py:98
  211.5 100.9 %all_to_all.10 = bf16[4,264,2048]{2,1,0:T(8,128)(2,1)} all-to-all(bf16[4,264,2048]{2,1,0:T(8,128)(2,1)S(1)} %bitcast.66), channel_id=1, replica_groups=mesh['req'=8,'head'=4] {'head'}, dimensions={0} | all-to-all | bytes 8650752 | tf_op jit(solution)/shard_map/all_to_all | solution.py:109
  312.4 3.2 reduce_sum.32
  315.6 1.4 add_convert_fusion
  (64 shorter events, 3.3 us)
Async XLA Ops:
  7.2 188.6 %all-gather.2.cloned.1.call-start = ((), (), s32[]{:S(2)}) async-start(), calls=%async_computation.2 | async-start | bytes 37748736 | tf_op jit(solution)/shard_map/all_gather | solution.py:100
  7.2 1.5 copy-start.10
  7.2 2.8 copy-start.9
  7.2 14.8 %copy-start.8 = (s32[2]{0:T(128)S(1)}, s32[2]{0:T(128)}, u32[]{:S(2)}) copy-start(s32[2]{0:T(128)} %refs_0_.1) | copy-start | bytes 28
  7.2 15.1 %copy-start = (s32[2,14]{1,0:T(2,128)S(1)}, s32[2,14]{1,0:T(2,128)}, u32[]{:S(2)}) copy-start(s32[2,14]{1,0:T(2,128)} %param.16) | copy-start | bytes 340
  7.9 19.3 %copy-start.4 = (bf16[28,128,256]{2,1,0:T(8,128)(2,1)S(1)}, bf16[28,128,256]{2,1,0:T(8,128)(2,1)}, u32[]{:S(2)}) copy-start(bf16[28,128,256]{2,1,0:T(8,128)(2,1)} %param.14) | copy-start | bytes 5505028
  7.9 19.3 %copy-start.6 = (bf16[512,256]{1,0:T(8,128)(2,1)S(1)}, bf16[512,256]{1,0:T(8,128)(2,1)}, u32[]{:S(2)}) copy-start(bf16[512,256]{1,0:T(8,128)(2,1)} %param.12) | copy-start | bytes 786436
  30.6 1.2 copy-start.3
  31.9 3.6 %copy-start.2 = (bf16[28,128,256]{2,1,0:T(8,128)(2,1)S(1)}, bf16[28,128,256]{2,1,0:T(8,128)(2,1)}, u32[]{:S(2)}) copy-start(bf16[28,128,256]{2,1,0:T(8,128)(2,1)} %param.15) | copy-start | bytes 5505028
  31.9 3.6 %copy-start.7 = (bf16[512,256]{1,0:T(8,128)(2,1)S(1)}, bf16[512,256]{1,0:T(8,128)(2,1)}, u32[]{:S(2)}) copy-start(bf16[512,256]{1,0:T(8,128)(2,1)} %param.13) | copy-start | bytes 786436
  39.0 1.9 copy-start.1
  92.2 53.0 %all-to-all-start = ((bf16[8,64,2048]{2,1,0:T(8,128)(2,1)}), bf16[8,64,2048]{2,1,0:T(8,128)(2,1)S(1)}, u32[]{:S(2)}, u32[]{:S(2)}) async-start(bf16[8,64,2048]{2,1,0:T(8,128)(2,1)} %select_select_fusion), calls=%async_computation | async-start | bytes 4194304 | tf_op jit(solution)/shard_map/all_to_all | solution.py:88
  312.4 3.2 copy-start.5
Sparse Core Ops, SparseCore 0:
  9.9 185.8 all-gather.1

commit v9 on v6

--- a/solution.py
+++ b/solution.py
@@ -94,12 +94,6 @@
     return blank_rows.at[landing.reshape(-1)].set(arrived.reshape(-1, columns), mode="drop")
 
 
-def project(row_block, out_weight):
-    blocks = lax.all_gather(out_weight, "req", axis=0, tiled=False)
-    product = jnp.einsum("rk,ckn->rcn", row_block, blocks, preferred_element_type=jnp.float32)
-    return product.reshape(row_block.shape[0], -1)
-
-
 def head_total(partial_sum):
     return lax.psum_scatter(
         partial_sum.astype(jnp.bfloat16), "head", scatter_dimension=1, tiled=True
@@ -162,7 +156,14 @@
     shares = jnp.maximum((totals[:, None] - lead_in + groups - 1) // groups, 0)
     starts = jnp.cumsum(shares, axis=0) - shares
     placed = deal(attended, new_counts, lead_in, shares, starts, totals, balanced)
-    summed = head_total(project(placed, out_weight)).astype(jnp.bfloat16)
+    weight_all = lax.all_gather(out_weight, "req", axis=1, tiled=True)
+    lead_rows = 40
+    summed = jnp.concatenate(
+        [
+            head_total(jnp.dot(piece, weight_all, preferred_element_type=jnp.float32))
+            for piece in (placed[:lead_rows], placed[lead_rows:])
+        ]
+    ).astype(jnp.bfloat16)
     hidden = (residual.astype(jnp.float32) + summed.astype(jnp.float32)).astype(jnp.bfloat16)
     return (hidden, gathered_keys, gathered_values)
 

time: 302 us -> 312 us (1.033)
  matrix products: 15.2 us -> 30.3 us
    dot_general x1 -> x2, matrix products: 15.2 us -> 30.3 us  [local(): jnp.dot(piece, weight_all, preferred_element_type=jnp.float32)]
    reduce_scatter x1 -> x2, waiting for transfers between devices: 79.1 us -> 76.3 us  [head_total(): lax.psum_scatter(partial_sum.astype(jnp.bfloat16), 'head', scatter_dimens...]
  transfers between devices with their start and end apart: 3 -> 4, of which waited for: 3 -> 4; matrix products, arithmetic and copies ran while one was open for 12% -> 17% of each run, Pallas kernels for 13% -> 12%
where the time goes in v9:
time: 312 us
  waiting for transfers between devices  172 us (55%)
  Pallas kernels  38.5 us (12%)
  local copies, waits for them, and re-layouts  35 us (11%)
  matrix products  30.3 us (10%)
  between operations  15.5 us (5%)
  blocking collectives  9.49 us (3%)
  other arithmetic  6.47 us (2%)
  starting transfers between devices  3.94 us (1%)
    reduce_scatter x2, waiting for transfers between devices, head_total(): lax.psum_scatter(partial_sum.astype(jnp.bfloat16), 'head', scatter_dimens...  76.3 us
    all_to_all x1, waiting for transfers between devices, deal(): lax.all_to_all(outgoing, 'req', split_axis=0, concat_axis=0, tiled=True)  48.8 us
    all_gather x1, waiting for transfers between devices, local(): weight_all = lax.all_gather(out_weight, 'req', axis=1, tiled=True)  46.7 us
    pallas_call x1, Pallas kernels, paged_attention(): pl.pallas_call(kernel, grid_spec=pltpu.PrefetchScalarGridSpec(num_scalar_...  38.5 us
    dot_general x2, matrix products, local(): jnp.dot(piece, weight_all, preferred_element_type=jnp.float32)  30.3 us
    unnamed x1, blocking collectives  9.49 us
    gather x1, local copies, waits for them, and re-layouts, deal(): jnp.take(row_block, source.reshape(-1), axis=0)  6.27 us
  transfers between devices with their start and end apart: 4, of which 4 were waited for; matrix products, arithmetic and copies ran while one was open for 17% of the time, Pallas kernels for 12%

profile of v9, /device:TPU:0, one launch (start us, length us, event | category | flops | bytes accessed | tf_op | source)
XLA Modules:
  0.0 311.6 jit_solution(15187882182919016121)
XLA Ops:
  7.3 0.6 all-gather.2.cloned.1.call-update
  10.2 0.8 dynamic-update-slice.1
  11.0 9.5 %all-reduce.2 = (s32[16]{0:T(128)S(1)}, s32[8]{0:T(128)S(1)}) all-reduce(s32[16]{0:T(128)S(1)} %dynamic-update-slice, s32[8]{0:T(128)S(1)} %dynamic-update-slice.1), channel_id=1, replica_groups=mesh['req'=8,'head'=4] {'req'}, use_global_device_ids=true, to_apply=%add | all-reduce | flops 24 | bytes 192
  22.3 4.8 %gather_fusion.4 = s32[512]{0:T(512)S(1)} fusion(s32[2,14]{1,0:T(2,128)S(1)} %copy-done, s32[512]{0:T(512)S(1)} %bitcast.52), kind=kCustom, calls=%fused_computation.4 | custom fusion | bytes 8192 | tf_op jit(solution)/shard_map/jit(take_along_axis)/gather | solution.py:129
  27.3 3.4 %scatter_fusion = bf16[3584,256]{1,0:T(8,128)(2,1)S(1)} fusion(bf16[3584,256]{1,0:T(8,128)(2,1)S(1)} %bitcast.58, s32[512]{0:T(512)S(1)} %bitcast.64, bf16[512,256]{1,0:T(8,128)(2,1)S(1)} %copy-done.6), kind=kCustom, calls=%fused_computation.5 | custom fusion | bytes 788480 | tf_op jit(solution)/shard_map/scatter | solution.py:136
  30.7 1.2 copy-done.3
  31.9 3.6 %gather_fusion.1 = bf16[28,128,256]{2,1,0:T(8,128)(2,1)} fusion(bf16[28,128,256]{2,1,0:T(8,128)(2,1)} %bitcast.56, s32[1024]{0:T(1024)S(1)} %pad_clamp_fusion.1), kind=kCustom, calls=%fused_computation.1 | custom fusion | bytes 3670128 | tf_op jit(solution)/shard_map/gather | solution.py:144
  35.5 3.6 %scatter_fusion.1 = bf16[3584,256]{1,0:T(8,128)(2,1)S(1)} fusion(bf16[3584,256]{1,0:T(8,128)(2,1)S(1)} %bitcast.55, s32[512]{0:T(512)S(1)} %bitcast.65, bf16[512,256]{1,0:T(8,128)(2,1)S(1)} %copy-done.7), kind=kCustom, calls=%fused_computation.6 | custom fusion | bytes 788480 | tf_op jit(solution)/shard_map/scatter | solution.py:138
  39.1 1.9 gather_fusion.2
  41.0 3.3 %gather_fusion = s32[512]{0:T(512)S(1)} fusion(s32[2]{0:T(128)S(1)} %bitcast_subtract_fusion, s32[1024]{0:T(1024)S(1)} %pad_clamp_fusion.2), kind=kCustom, calls=%fused_computation | custom fusion | bytes 6144 | tf_op jit(solution)/shard_map/jit(_take)/gather | solution.py:82
  44.4 38.5 %shard_map.130 = bf16[512,2048]{1,0:T(8,128)(2,1)} custom-call(s32[2]{0:T(128)} %refs_0_.1, bf16[512,2048]{1,0:T(8,128)(2,1)} %refs_1_.1, bf16[2,1792,256]{2,1,0:T(8,128)(2,1)} %bitcast.60, bf16[2,1792,256]{2,1,0:T(8,128)(2,1)} %bitcast.61), custom_call_target="tpu_custom_call" | custom-call | tf_op jit(solution)/shard_map/pallas_call | solution.py:48
  82.9 0.7 compare_select_fusion
  83.6 6.3 %gather_fusion.3 = bf16[512,2048]{1,0:T(8,128)(2,1)S(1)} fusion(bf16[512,2048]{1,0:T(8,128)(2,1)} %shard_map.130, s32[1024]{0:T(1024)S(1)} %pad_clamp_fusion), kind=kCustom, calls=%fused_computation.3 | custom fusion | bytes 4196352 | tf_op jit(solution)/shard_map/jit(_take)/gather | solution.py:86
  89.9 0.7 add_compare_fusion
  90.6 1.6 select_select_fusion
  92.2 3.6 %all-to-all-start = ((bf16[8,64,2048]{2,1,0:T(8,128)(2,1)}), bf16[8,64,2048]{2,1,0:T(8,128)(2,1)S(1)}, u32[]{:S(2)}, u32[]{:S(2)}) async-start(bf16[8,64,2048]{2,1,0:T(8,128)(2,1)} %select_select_fusion), calls=%async_computation | async-start | bytes 4194304 | tf_op jit(solution)/shard_map/all_to_all | solution.py:88
  96.5 48.8 %all-to-all-done = bf16[8,64,2048]{2,1,0:T(8,128)(2,1)S(1)} async-done(((bf16[8,64,2048]{2,1,0:T(8,128)(2,1)}), bf16[8,64,2048]{2,1,0:T(8,128)(2,1)S(1)}, u32[]{:S(2)}, u32[]{:S(2)}) %all-to-all-start) | async-done | bytes 2097184 | tf_op jit(solution)/shard_map/all_to_all | solution.py:88
  145.2 3.8 %scatter_custom_fusion.2 = bf16[264,2048]{1,0:T(8,128)(2,1)S(1)} fusion(s32[512]{0:T(512)S(1)} %bitcast.72, bf16[512,2048]{1,0:T(8,128)(2,1)S(1)} %bitcast.62, bf16[]{:T(256)} %constant.123.clone.1), kind=kCustom, calls=%fused_computation.13 | custom fusion | bytes 1081346 | tf_op jit(solution)/shard_map/scatter | solution.py:94
  149.0 46.7 %all-gather.2.cloned.1.call-done = bf16[2048,8192]{1,0:T(8,128)(2,1)} async-done(((bf16[2048,1024]{1,0:T(8,128)(2,1)}), bf16[2048,8192]{1,0:T(8,128)(2,1)}) %all-gather.2.cloned.1.call-update) | async-done | bytes 33554448 | tf_op jit(solution)/shard_map/all_gather | solution.py:159
  195.8 14.4 %convolution_convert_fusion.1 = bf16[40,8192]{1,0:T(8,128)(2,1)} fusion(bf16[2048,8192]{1,0:T(8,128)(2,1)} %all-gather.2.cloned.1.call-done, bf16[264,2048]{1,0:T(8,128)(2,1)S(1)} %scatter_custom_fusion.2), kind=kOutput, calls=%fused_computation.9 | convolution fusion | flops 1342504960 | bytes 34373632 | tf_op jit(solution)/shard_map/dot_general | solution.py:163
  210.3 15.9 %convolution_convert_fusion = bf16[224,8192]{1,0:T(8,128)(2,1)} fusion(bf16[2048,8192]{1,0:T(8,128)(2,1)} %all-gather.2.cloned.1.call-done, bf16[264,2048]{1,0:T(8,128)(2,1)S(1)} %scatter_custom_fusion.2), kind=kOutput, calls=%fused_computation.8 | convolution fusion | flops 7518027776 | bytes 38141952 | tf_op jit(solution)/shard_map/dot_general | solution.py:163
  226.2 6.8 %reduce-scatter.3.cloned.1.call-done = bf16[40,2048]{1,0:T(8,128)(2,1)} async-done(((bf16[40,8192]{1,0:T(8,128)(2,1)}), bf16[40,2048]{1,0:T(8,128)(2,1)}) %reduce-scatter.3.cloned.1.call-update) | async-done | bytes 163856 | tf_op jit(solution)/shard_map/reduce_scatter | solution.py:98
  233.0 69.6 %reduce-scatter.5.cloned.1.call-done = bf16[224,2048]{1,0:T(8,128)(2,1)} async-done(((bf16[224,8192]{1,0:T(8,128)(2,1)}), bf16[224,2048]{1,0:T(8,128)(2,1)}) %reduce-scatter.5.cloned.1.call-update) | async-done | bytes 917520 | tf_op jit(solution)/shard_map/reduce_scatter | solution.py:98
  302.5 2.6 add_convert_fusion
  (68 shorter events, 3.7 us)
Async XLA Ops:
  7.2 188.6 %all-gather.2.cloned.1.call-start = ((), (), s32[]{:S(2)}) async-start(), calls=%async_computation.3 | async-start | bytes 37748736 | tf_op jit(solution)/shard_map/all_gather | solution.py:159
  7.2 1.5 copy-start.10
  7.2 2.8 copy-start.9
  7.2 14.8 %copy-start.8 = (s32[2]{0:T(128)S(1)}, s32[2]{0:T(128)}, u32[]{:S(2)}) copy-start(s32[2]{0:T(128)} %refs_0_.1) | copy-start | bytes 28
  7.2 15.1 %copy-start = (s32[2,14]{1,0:T(2,128)S(1)}, s32[2,14]{1,0:T(2,128)}, u32[]{:S(2)}) copy-start(s32[2,14]{1,0:T(2,128)} %param.16) | copy-start | bytes 340
  7.9 19.3 %copy-start.4 = (bf16[28,128,256]{2,1,0:T(8,128)(2,1)S(1)}, bf16[28,128,256]{2,1,0:T(8,128)(2,1)}, u32[]{:S(2)}) copy-start(bf16[28,128,256]{2,1,0:T(8,128)(2,1)} %param.14) | copy-start | bytes 5505028
  7.9 19.3 %copy-start.6 = (bf16[512,256]{1,0:T(8,128)(2,1)S(1)}, bf16[512,256]{1,0:T(8,128)(2,1)}, u32[]{:S(2)}) copy-start(bf16[512,256]{1,0:T(8,128)(2,1)} %param.12) | copy-start | bytes 786436
  30.6 1.2 copy-start.3
  31.9 3.6 %copy-start.2 = (bf16[28,128,256]{2,1,0:T(8,128)(2,1)S(1)}, bf16[28,128,256]{2,1,0:T(8,128)(2,1)}, u32[]{:S(2)}) copy-start(bf16[28,128,256]{2,1,0:T(8,128)(2,1)} %param.15) | copy-start | bytes 5505028
  31.9 3.6 %copy-start.7 = (bf16[512,256]{1,0:T(8,128)(2,1)S(1)}, bf16[512,256]{1,0:T(8,128)(2,1)}, u32[]{:S(2)}) copy-start(bf16[512,256]{1,0:T(8,128)(2,1)} %param.13) | copy-start | bytes 786436
  39.0 1.9 copy-start.1
  92.2 53.0 %all-to-all-start = ((bf16[8,64,2048]{2,1,0:T(8,128)(2,1)}), bf16[8,64,2048]{2,1,0:T(8,128)(2,1)S(1)}, u32[]{:S(2)}, u32[]{:S(2)}) async-start(bf16[8,64,2048]{2,1,0:T(8,128)(2,1)} %select_select_fusion), calls=%async_computation | async-start | bytes 4194304 | tf_op jit(solution)/shard_map/all_to_all | solution.py:88
  95.8 137.1 %reduce-scatter.3.cloned.1.call-start = ((), (), s32[]{:S(2)}) async-start(), calls=%async_computation.4 | async-start | bytes 819200 | tf_op jit(solution)/shard_map/reduce_scatter | solution.py:98
  210.2 92.3 %reduce-scatter.5.cloned.1.call-start = ((), (), s32[]{:S(2)}) async-start(), calls=%async_computation.5 | async-start | bytes 4587520 | tf_op jit(solution)/shard_map/reduce_scatter | solution.py:98
  226.1 76.4 %copy-start.5 = (bf16[264,2048]{1,0:T(8,128)(2,1)S(1)}, bf16[264,2048]{1,0:T(8,128)(2,1)}, u32[]{:S(2)}) copy-start(bf16[264,2048]{1,0:T(8,128)(2,1)} %param.20) | copy-start | bytes 3244036
Sparse Core Ops, SparseCore 0:
  9.9 185.8 all-gather.1
  210.3 22.5 reduce-scatter.2
  235.3 67.2 reduce-scatter.4

commit v10 on v2

--- a/solution.py
+++ b/solution.py
@@ -164,8 +164,13 @@
     shares = jnp.maximum((totals[:, None] - lead_in + groups - 1) // groups, 0)
     starts = jnp.cumsum(shares, axis=0) - shares
     placed = deal(attended, new_counts, lead_in, shares, starts, totals, balanced)
-    summed = head_total(project(placed, out_weight)).astype(jnp.bfloat16)
-    hidden = (residual.astype(jnp.float32) + summed.astype(jnp.float32)).astype(jnp.bfloat16)
+    partial_sum = project(placed, out_weight)
+    width = residual.shape[1]
+    own_cols = lax.axis_index("head") * width
+    own_part = lax.dynamic_slice_in_dim(partial_sum, own_cols, width, 1)
+    own_part = own_part.astype(jnp.bfloat16).astype(jnp.float32) + residual.astype(jnp.float32)
+    partial_sum = lax.dynamic_update_slice_in_dim(partial_sum, own_part, own_cols, 1)
+    hidden = head_total(partial_sum).astype(jnp.bfloat16)
     return (hidden, gathered_keys, gathered_values)
 
 

time: 301 us -> 301 us (level)
  no operation moved by 1% of the time
where the time goes in v10:
time: 301 us
  waiting for transfers between devices  175 us (58%)
  Pallas kernels  38.5 us (13%)
  local copies, waits for them, and re-layouts  35 us (12%)
  matrix products  16.5 us (5%)
  between operations  15.6 us (5%)
  blocking collectives  9.49 us (3%)
  other arithmetic  6.55 us (2%)
  starting transfers between devices  3.9 us (1%)
    reduce_scatter x1, waiting for transfers between devices, head_total(): lax.psum_scatter(partial_sum.astype(jnp.bfloat16), 'head', scatter_dimens...  79 us
    all_to_all x1, waiting for transfers between devices, deal(): lax.all_to_all(outgoing, 'req', split_axis=0, concat_axis=0, tiled=True)  48.8 us
    all_gather x1, waiting for transfers between devices, project(): lax.all_gather(out_weight, 'req', axis=1, tiled=True)  46.9 us
    pallas_call x1, Pallas kernels, paged_attention(): pl.pallas_call(kernel, grid_spec=pltpu.PrefetchScalarGridSpec(num_scalar_...  38.5 us
    dot_general x1, matrix products, project(): jnp.dot(row_block, lax.all_gather(out_weight, 'req', axis=1, tiled=True),...  16.5 us
    unnamed x1, blocking collectives  9.49 us
    gather x1, local copies, waits for them, and re-layouts, deal(): jnp.take(row_block, source.reshape(-1), axis=0)  6.27 us
  transfers between devices with their start and end apart: 3, of which 3 were waited for; matrix products, arithmetic and copies ran while one was open for 13% of the time, Pallas kernels for 13%

profile of v10, /device:TPU:0, one launch (start us, length us, event | category | flops | bytes accessed | tf_op | source)
XLA Modules:
  0.0 300.9 jit_solution(2368230597483501106)
XLA Ops:
  7.3 0.6 all-gather.2.cloned.1.call-update
  8.6 0.6 dynamic-slice
  10.1 0.8 dynamic-update-slice.1
  10.8 9.5 %all-reduce.2 = (s32[16]{0:T(128)S(1)}, s32[8]{0:T(128)S(1)}) all-reduce(s32[16]{0:T(128)S(1)} %dynamic-update-slice, s32[8]{0:T(128)S(1)} %dynamic-update-slice.1), channel_id=1, replica_groups=mesh['req'=8,'head'=4] {'req'}, use_global_device_ids=true, to_apply=%add | all-reduce | flops 24 | bytes 192
  20.8 0.6 dynamic_slice.21
  22.2 4.8 %gather_fusion.4 = s32[512]{0:T(512)S(1)} fusion(s32[2,14]{1,0:T(2,128)S(1)} %copy-done, s32[512]{0:T(512)S(1)} %bitcast.52), kind=kCustom, calls=%fused_computation.4 | custom fusion | bytes 8192 | tf_op jit(solution)/shard_map/jit(take_along_axis)/gather | solution.py:137
  27.1 3.3 %gather_fusion = s32[512]{0:T(512)S(1)} fusion(s32[2]{0:T(128)S(1)} %bitcast_subtract_fusion, s32[1024]{0:T(1024)S(1)} %pad_clamp_fusion.2), kind=kCustom, calls=%fused_computation | custom fusion | bytes 6144 | tf_op jit(solution)/shard_map/jit(_take)/gather | solution.py:82
  30.5 0.7 compare_select_fusion
  31.2 3.4 %scatter_fusion.1 = bf16[3584,256]{1,0:T(8,128)(2,1)S(1)} fusion(bf16[3584,256]{1,0:T(8,128)(2,1)S(1)} %bitcast.58, s32[512]{0:T(512)S(1)} %bitcast.64, bf16[512,256]{1,0:T(8,128)(2,1)S(1)} %copy-done.6), kind=kCustom, calls=%fused_computation.6 | custom fusion | bytes 788480 | tf_op jit(solution)/shard_map/scatter | solution.py:146
  34.6 1.2 copy-done.3
  35.8 3.6 %gather_fusion.2 = bf16[28,128,256]{2,1,0:T(8,128)(2,1)} fusion(bf16[28,128,256]{2,1,0:T(8,128)(2,1)} %bitcast.56, s32[1024]{0:T(1024)S(1)} %pad_clamp_fusion.1), kind=kCustom, calls=%fused_computation.2 | custom fusion | bytes 3670128 | tf_op jit(solution)/shard_map/gather | solution.py:153
  39.4 3.6 %scatter_fusion = bf16[3584,256]{1,0:T(8,128)(2,1)S(1)} fusion(bf16[3584,256]{1,0:T(8,128)(2,1)S(1)} %bitcast.55, s32[512]{0:T(512)S(1)} %bitcast.65, bf16[512,256]{1,0:T(8,128)(2,1)S(1)} %copy-done.7), kind=kCustom, calls=%fused_computation.5 | custom fusion | bytes 788480 | tf_op jit(solution)/shard_map/scatter | solution.py:144
  43.0 1.9 gather_fusion.1
  44.9 38.5 %shard_map.130 = bf16[512,2048]{1,0:T(8,128)(2,1)} custom-call(s32[2]{0:T(128)} %refs_0_.1, bf16[512,2048]{1,0:T(8,128)(2,1)} %refs_1_.1, bf16[2,1792,256]{2,1,0:T(8,128)(2,1)} %bitcast.61, bf16[2,1792,256]{2,1,0:T(8,128)(2,1)} %bitcast.60), custom_call_target="tpu_custom_call" | custom-call | tf_op jit(solution)/shard_map/pallas_call | solution.py:48
  83.4 6.3 %gather_fusion.3 = bf16[512,2048]{1,0:T(8,128)(2,1)S(1)} fusion(bf16[512,2048]{1,0:T(8,128)(2,1)} %shard_map.130, s32[1024]{0:T(1024)S(1)} %pad_clamp_fusion), kind=kCustom, calls=%fused_computation.3 | custom fusion | bytes 4196352 | tf_op jit(solution)/shard_map/jit(_take)/gather | solution.py:86
  89.7 0.7 add_compare_fusion
  90.4 1.6 select_select_fusion
  92.1 3.6 %all-to-all-start = ((bf16[8,64,2048]{2,1,0:T(8,128)(2,1)}), bf16[8,64,2048]{2,1,0:T(8,128)(2,1)S(1)}, u32[]{:S(2)}, u32[]{:S(2)}) async-start(bf16[8,64,2048]{2,1,0:T(8,128)(2,1)} %select_select_fusion), calls=%async_computation | async-start | bytes 4194304 | tf_op jit(solution)/shard_map/all_to_all | solution.py:88
  96.3 48.8 %all-to-all-done = bf16[8,64,2048]{2,1,0:T(8,128)(2,1)S(1)} async-done(((bf16[8,64,2048]{2,1,0:T(8,128)(2,1)}), bf16[8,64,2048]{2,1,0:T(8,128)(2,1)S(1)}, u32[]{:S(2)}, u32[]{:S(2)}) %all-to-all-start) | async-done | bytes 2097184 | tf_op jit(solution)/shard_map/all_to_all | solution.py:88
  145.1 3.8 %scatter_custom_fusion.2 = bf16[264,2048]{1,0:T(8,128)(2,1)S(1)} fusion(s32[512]{0:T(512)S(1)} %bitcast.72, bf16[512,2048]{1,0:T(8,128)(2,1)S(1)} %bitcast.62, bf16[]{:T(256)} %constant.127.clone.1), kind=kCustom, calls=%fused_computation.11 | custom fusion | bytes 1081346 | tf_op jit(solution)/shard_map/scatter | solution.py:94
  148.9 46.9 %all-gather.2.cloned.1.call-done = bf16[2048,8192]{1,0:T(8,128)(2,1)} async-done(((bf16[2048,1024]{1,0:T(8,128)(2,1)}), bf16[2048,8192]{1,0:T(8,128)(2,1)}) %all-gather.2.cloned.1.call-update) | async-done | bytes 33554448 | tf_op jit(solution)/shard_map/all_gather | solution.py:100
  195.8 16.5 %fusion.18 = bf16[264,8192]{1,0:T(8,128)(2,1)} fusion(bf16[264,2048]{1,0:T(8,128)(2,1)S(1)} %scatter_custom_fusion.2, bf16[2048,8192]{1,0:T(8,128)(2,1)} %all-gather.2.cloned.1.call-done), kind=kOutput, calls=%fused_computation.82 | convolution fusion | flops 8858370048 | bytes 38961152 | tf_op jit(solution)/shard_map/dot_general | solution.py:98
  212.3 2.7 add_dynamic-update-slice_fusion
  215.0 79.0 %reduce-scatter.2.cloned.1.call-done = bf16[264,2048]{1,0:T(8,128)(2,1)} async-done(((bf16[264,8192]{1,0:T(8,128)(2,1)}), bf16[264,2048]{1,0:T(8,128)(2,1)}) %reduce-scatter.2.cloned.1.call-update) | async-done | bytes 1081360 | tf_op jit(solution)/shard_map/reduce_scatter | solution.py:106
  (63 shorter events, 2.4 us)
Async XLA Ops:
  7.2 188.6 %all-gather.2.cloned.1.call-start = ((), (), s32[]{:S(2)}) async-start(), calls=%async_computation.2 | async-start | bytes 37748736 | tf_op jit(solution)/shard_map/all_gather | solution.py:100
  7.2 1.3 copy-start.10
  7.2 2.6 copy-start.9
  7.2 14.7 %copy-start.8 = (s32[2]{0:T(128)S(1)}, s32[2]{0:T(128)}, u32[]{:S(2)}) copy-start(s32[2]{0:T(128)} %refs_0_.1) | copy-start | bytes 28
  7.2 14.9 %copy-start = (s32[2,14]{1,0:T(2,128)S(1)}, s32[2,14]{1,0:T(2,128)}, u32[]{:S(2)}) copy-start(s32[2,14]{1,0:T(2,128)} %param.16) | copy-start | bytes 340
  27.1 4.1 %copy-start.4 = (bf16[28,128,256]{2,1,0:T(8,128)(2,1)S(1)}, bf16[28,128,256]{2,1,0:T(8,128)(2,1)}, u32[]{:S(2)}) copy-start(bf16[28,128,256]{2,1,0:T(8,128)(2,1)} %param.15) | copy-start | bytes 5505028
  27.1 4.1 %copy-start.6 = (bf16[512,256]{1,0:T(8,128)(2,1)S(1)}, bf16[512,256]{1,0:T(8,128)(2,1)}, u32[]{:S(2)}) copy-start(bf16[512,256]{1,0:T(8,128)(2,1)} %param.13) | copy-start | bytes 786436
  34.6 1.2 copy-start.3
  35.8 3.6 %copy-start.2 = (bf16[28,128,256]{2,1,0:T(8,128)(2,1)S(1)}, bf16[28,128,256]{2,1,0:T(8,128)(2,1)}, u32[]{:S(2)}) copy-start(bf16[28,128,256]{2,1,0:T(8,128)(2,1)} %param.14) | copy-start | bytes 5505028
  35.8 3.6 %copy-start.7 = (bf16[512,256]{1,0:T(8,128)(2,1)S(1)}, bf16[512,256]{1,0:T(8,128)(2,1)}, u32[]{:S(2)}) copy-start(bf16[512,256]{1,0:T(8,128)(2,1)} %param.12) | copy-start | bytes 786436
  43.0 2.0 copy-start.1
  92.1 53.0 %all-to-all-start = ((bf16[8,64,2048]{2,1,0:T(8,128)(2,1)}), bf16[8,64,2048]{2,1,0:T(8,128)(2,1)S(1)}, u32[]{:S(2)}, u32[]{:S(2)}) async-start(bf16[8,64,2048]{2,1,0:T(8,128)(2,1)} %select_select_fusion), calls=%async_computation | async-start | bytes 4194304 | tf_op jit(solution)/shard_map/all_to_all | solution.py:88
  95.7 198.3 %reduce-scatter.2.cloned.1.call-start = ((), (), s32[]{:S(2)}) async-start(), calls=%async_computation.3 | async-start | bytes 5406720 | tf_op jit(solution)/shard_map/reduce_scatter | solution.py:106
  148.9 63.4 %copy-start.5 = (bf16[264,2048]{1,0:T(8,128)(2,1)S(1)}, bf16[264,2048]{1,0:T(8,128)(2,1)}, u32[]{:S(2)}) copy-start(bf16[264,2048]{1,0:T(8,128)(2,1)} %param.20) | copy-start | bytes 3244036
Sparse Core Ops, SparseCore 0:
  9.9 185.8 all-gather.1
  215.1 78.8 reduce-scatter.1
